TPU v7x, 256 devices: a whole 4x4x8 slice. The times are simulated.
256 devices in a mesh: seq: 8 (over z), exp: 8 (over x, y_hi), img: 4 (over y_lo, core).
Axes of the slice: x: 4, y: 4 (y_hi: 2, y_lo: 2; y = y_hi * 2 + y_lo), z: 8, core: 2. Of those that a mesh axis runs over, the one named last changes fastest.
Arguments:
- projected: bfloat16 [32, 1024, 3, 1280], P(('img', 'exp'), 'seq'), parts along dimension 0, may hold values from -6 to 6
- residual: bfloat16 [32, 1024, 1280], P(('img', 'exp'), 'seq'), parts along dimension 0, may hold values from -6 to 6
- attn_proj: bfloat16 [1280, 1280], P('seq'), may hold values from -0.15625 to 0.15625
- norm_gain: float32 [1280], replicated, may hold values from 0.5 to 2
- norm_bias: float32 [1280], replicated, may hold values from -3 to 3
- expert_ids: int32 [32, 1024, 1], P(('img', 'exp')), parts along dimension 0, may hold values from 0 to 15; in each aligned block of 128 rows (0 to 127, 128 to 255, ..., all dimensions but the last counted through in order) at most 12 rows name the same one
- expert_up: bfloat16 [16, 1280, 5120], P('exp', None, 'seq'), may hold values from -0.15625 to 0.15625
- expert_down: bfloat16 [16, 5120, 1280], P('exp', 'seq'), may hold values from -0.078125 to 0.078125
Outputs:
- layer_out: bfloat16 [32, 1024, 1280], P(('img', 'exp'), 'seq'), parts along dimension 0
There are 4 independent parts, one for each index of `img`. A program takes and returns all parts, laid end to end along the dimension named above; an argument that names none is the same for every part. Nothing has to cross between parts.
Inputs may be any that keep to these rules, and one draw needn't show every extreme that they name: `expert_ids`: in each sequence, within every aligned block of 128 tokens, no expert is named by more than 12 tokens.
All inputs are finite; a program needn't handle non-finite values.
Results may differ from a plain program's by a relative error of at most 0.015.
Values may be sent and summed in bfloat16 or wider, within the bound.
No kernel may reach another device: no remote copies, remote signals or barrier semaphores. Data moves between devices by JAX's collectives and lax.ppermute only.
A program may use at most 64 MiB of HBM per device.

v0:
```python
import jax
import jax.numpy as jnp
from jax import lax
from jax.sharding import PartitionSpec as P

HEADS = 16
HEAD_DIM = 80


def attend(gathered):
    queries = gathered[:, 0, 0]
    keys_all = gathered[:, 1, 0]
    values = gathered[:, 2, 0]
    length = queries.shape[0]
    span_rows = length
    factor = 1.0 / queries.shape[2] ** 0.5

    def one_block(offset):
        query_rows = lax.dynamic_slice_in_dim(queries, offset, span_rows, 0)
        scores = (
            jnp.einsum("qhd,khd->hqk", query_rows, keys_all, preferred_element_type=jnp.float32)
            * factor
        )
        peak = jnp.max(scores, axis=-1, keepdims=True)
        powers = jnp.exp(scores - peak)
        weights = (powers / jnp.sum(powers, axis=-1, keepdims=True)).astype(jnp.bfloat16)
        mixed = jnp.einsum("hqk,khd->qhd", weights, values, preferred_element_type=jnp.float32)
        return mixed.astype(jnp.bfloat16)

    starts = jnp.arange(length // span_rows, dtype=jnp.int32) * span_rows
    blocks = lax.map(one_block, starts)
    return blocks.reshape(length, queries.shape[1], queries.shape[2])


def layer_norm(stream, norm_gain, norm_bias):
    values = stream.astype(jnp.float32)
    centre = jnp.mean(values, axis=-1, keepdims=True)
    centered = values - centre
    variance = jnp.mean(centered * centered, axis=-1, keepdims=True)
    return (centered / jnp.sqrt(variance + 1e-06) * norm_gain + norm_bias).astype(jnp.bfloat16)


def per_device(
    projected, residual, attn_proj, norm_gain, norm_bias, expert_ids, expert_up, expert_down
):
    tok_rows = projected.shape[1]
    model_width = projected.shape[3]
    seq_count = lax.axis_size("seq")
    exp_count = lax.axis_size("exp")
    local_experts = expert_up.shape[0]
    experts = local_experts * exp_count
    cap_dev = 3 * tok_rows // (2 * experts)
    capacity = cap_dev * seq_count
    length = tok_rows * seq_count
    heads_here = HEADS // seq_count
    head_width = heads_here * HEAD_DIM
    regrouped = projected[0].reshape(tok_rows, 3, seq_count, heads_here, HEAD_DIM)
    attended = attend(lax.all_to_all(regrouped, "seq", split_axis=2, concat_axis=0, tiled=True))
    attended = attended.reshape(seq_count, tok_rows, 1, head_width)
    token_heads = lax.all_to_all(attended, "seq", split_axis=0, concat_axis=2, tiled=True).reshape(
        tok_rows, model_width
    )
    projected_sum = jnp.dot(
        token_heads,
        lax.all_gather(attn_proj, "seq", axis=0, tiled=True),
        preferred_element_type=jnp.float32,
    )
    stream_own = residual[0].astype(jnp.float32) + projected_sum
    stream = stream_own.astype(jnp.bfloat16)
    stream_own = stream.astype(jnp.float32)
    normed = layer_norm(stream, norm_gain, norm_bias)
    seq_index = lax.axis_index("seq")
    ids_own = lax.dynamic_slice_in_dim(expert_ids[0, :, 0], seq_index * tok_rows, tok_rows)
    onehot = (ids_own[:, None] == jnp.arange(experts, dtype=jnp.int32)[None, :]).astype(jnp.int32)
    before = jnp.cumsum(onehot, axis=0) - onehot
    order_in_block = jnp.sum(before * onehot, axis=1)
    dest = ids_own * cap_dev + order_in_block
    select = (dest[:, None] == jnp.arange(experts * cap_dev, dtype=jnp.int32)[None, :]).astype(
        jnp.bfloat16
    )
    dispatch = jnp.einsum(
        "tk,td->kd", select, normed, preferred_element_type=jnp.float32
    ).astype(jnp.bfloat16)
    dispatch = dispatch.reshape(exp_count, local_experts, cap_dev, model_width)
    arrived = lax.all_to_all(dispatch, "exp", split_axis=0, concat_axis=0, tiled=True)
    gathered = lax.all_gather(arrived, "seq", axis=0, tiled=False)
    hidden = jax.nn.gelu(
        jnp.einsum("sejcd,jdf->sejcf", gathered, expert_up, preferred_element_type=jnp.float32),
        approximate=False,
    ).astype(jnp.bfloat16)
    pieces = jnp.einsum(
        "sejcf,jfd->sejcd", hidden, expert_down, preferred_element_type=jnp.float32
    ).astype(jnp.bfloat16)
    summed = lax.psum_scatter(pieces, "seq", scatter_dimension=0, tiled=True)[0]
    returned = lax.all_to_all(summed, "exp", split_axis=0, concat_axis=0, tiled=True).reshape(
        experts * cap_dev, model_width
    )
    expert_out = jnp.einsum("tk,kd->td", select, returned, preferred_element_type=jnp.float32)
    return (stream_own + expert_out).astype(jnp.bfloat16)[None]


def solution(mesh):
    return jax.shard_map(
        per_device,
        mesh=mesh,
        in_specs=(
            P(("img", "exp"), "seq", None, None),
            P(("img", "exp"), "seq", None),
            P("seq", None),
            P(),
            P(),
            P(("img", "exp"), None, None),
            P("exp", None, "seq"),
            P("exp", "seq", None),
        ),
        out_specs=P(("img", "exp"), "seq", None),
        check_vma=False,
    )
```

profile of v0, /device:TPU:8, one launch (start us, length us, event | category | flops | bytes accessed | tf_op | source)
XLA Modules:
  0.0 278.1 jit_solution(13850771605445924036)
XLA Ops:
  6.5 0.0 copy-start
  6.5 0.0 all-gather.4.cloned.1.call-start
  6.5 0.7 all-gather.4.cloned.1.call-update
  7.3 2.5 copy.18
  9.8 2.2 copy.19
  12.0 8.5 %all-to-all-start = ((bf16[128,3,8,2,80]{0,4,3,1,2:T(8,128)(2,1)}), bf16[128,3,8,2,80]{0,4,3,1,2:T(8,128)(2,1)}, u32[]{:S(2)}, u32[]{:S(2)}) async-start(bf16[128,3,8,2,80]{0,4,3,1,2:T(8,128)(2,1)} %copy.19), calls=%async_computation | async-start | bytes 1966080 | tf_op jit(solution)/shard_map/all_to_all | solution.py:58
  20.5 38.0 %all-to-all-done = bf16[128,3,8,2,80]{0,4,3,1,2:T(8,128)(2,1)} async-done(((bf16[128,3,8,2,80]{0,4,3,1,2:T(8,128)(2,1)}), bf16[128,3,8,2,80]{0,4,3,1,2:T(8,128)(2,1)}, u32[]{:S(2)}, u32[]{:S(2)}) %all-to-all-start) | async-done | bytes 983072 | tf_op jit(solution)/shard_map/all_to_all | solution.py:58
  58.4 2.6 copy.20
  61.0 2.3 all_to_all.33
  63.3 7.1 %fusion.87 = (f32[2,1024]{1,0:T(2,128)S(1)}, f32[2,1024,1024]{1,2,0:T(8,128)}) fusion(bf16[1024,3,1,2,80]{0,4,3,2,1:T(8,128)(2,1)} %all_to_all.33), kind=kOutput, calls=%fused_computation.107 | convolution fusion | flops 341836800 | bytes 9052160 | tf_op jit(solution)/shard_map/while/body/eval_jaxpr/sub | solution.py:25
  70.4 4.4 %fusion.49 = bf16[2,1024,80]{1,2,0:T(8,128)(2,1)S(1)} fusion(f32[2,1024,1024]{1,2,0:T(8,128)} %get-tuple-element.14, f32[2,1024]{1,0:T(2,128)S(1)} %get-tuple-element.13, bf16[1024,3,1,2,80]{0,4,3,2,1:T(8,128)(2,1)} %all_to_all.33), kind=kOutput, calls=%fused_computation.58 | convolution fusion | flops 339902464 | bytes 9052160 | tf_op jit(solution)/shard_map/while/body/eval_jaxpr/hqk,khd->qhd/dot_general | solution.py:27
  74.8 0.0 copy-start.2
  74.8 0.0 copy-start.3
  74.8 0.1 copy.31
  74.9 0.8 copy.22
  75.6 4.1 %all-to-all-start.1 = ((bf16[8,128,1,160]{1,3,2,0:T(8,128)(2,1)}), bf16[8,128,1,160]{1,3,2,0:T(8,128)(2,1)}, u32[]{:S(2)}, u32[]{:S(2)}) async-start(bf16[8,128,1,160]{1,3,2,0:T(8,128)(2,1)} %copy.22), calls=%async_computation.1 | async-start | bytes 655360 | tf_op jit(solution)/shard_map/all_to_all | solution.py:60
  79.7 0.0 all-gather.6.cloned.1.call-start
  79.8 0.7 dynamic-slice_bitcast_fusion
  80.4 0.1 fusion.55
  80.5 0.2 reduce_window_sum.11
  80.7 0.2 select_reduce_fusion
  80.9 0.7 multiply_add_fusion
  81.5 11.7 %all-to-all-done.1 = bf16[8,128,1,160]{1,3,2,0:T(8,128)(2,1)} async-done(((bf16[8,128,1,160]{1,3,2,0:T(8,128)(2,1)}), bf16[8,128,1,160]{1,3,2,0:T(8,128)(2,1)}, u32[]{:S(2)}, u32[]{:S(2)}) %all-to-all-start.1) | async-done | bytes 327712 | tf_op jit(solution)/shard_map/all_to_all | solution.py:60
  93.2 0.0 all-gather.4.cloned.1.call-done
  93.2 2.8 fusion.88
  96.0 0.0 copy-start.1
  96.0 0.2 multiply_reduce_fusion.1
  96.3 0.6 copy-done.1
  96.9 0.0 copy-done.2
  96.9 0.0 copy-done.3
  96.9 1.2 convolution_convert_fusion.1
  98.1 2.0 reshape.41
  100.1 1.5 copy.23
  101.5 16.4 %all_to_all.43 = bf16[8,2,12,1280]{3,1,2,0:T(2,128)(2,1)} all-to-all(bf16[8,2,12,1280]{3,1,2,0:T(2,128)(2,1)S(1)} %copy.23), channel_id=1, replica_groups=mesh['seq'=8,'exp'=8,'img'=4] {'exp'}, dimensions={0} | all-to-all | bytes 983040 | tf_op jit(solution)/shard_map/all_to_all | solution.py:85
  118.0 0.0 all-gather.6.cloned.1.call-update
  118.0 0.2 reduce-scatter.2.cloned.1.call-start
  118.2 45.5 %all-gather.6.cloned.1.call-done = bf16[64,2,12,1280]{3,1,2,0:T(2,128)(2,1)} async-done(((bf16[8,2,12,1280]{3,1,2,0:T(2,128)(2,1)}), bf16[64,2,12,1280]{3,1,2,0:T(2,128)(2,1)}) %all-gather.6.cloned.1.call-update) | async-done | bytes 3932176 | tf_op jit(solution)/shard_map/all_gather | solution.py:86
  163.7 5.2 %copy.24 = bf16[64,2,12,1280]{3,2,0,1:T(8,128)(2,1)} copy(bf16[64,2,12,1280]{3,1,2,0:T(2,128)(2,1)} %all-gather.6.cloned.1.call-done) | data formatting | bytes 7864320 | tf_op jit(solution)/shard_map/all_gather | solution.py:86
  168.8 0.0 copy-done
  168.8 22.1 %fusion.22 = bf16[8,8,2,12,1280]{4,3,1,0,2:T(8,128)(2,1)} fusion(bf16[2,640,1280]{2,1,0:T(8,128)(2,1)S(1)} %copy-done, bf16[8,8,2,12,1280]{4,3,1,0,2:T(8,128)(2,1)} %bitcast.141, bf16[2,1280,640]{2,1,0:T(8,128)(2,1)} %param.14), kind=kOutput, calls=%fused_computation.30 | convolution fusion | flops 5099028480 | bytes 14417920 | tf_op jit(solution)/shard_map/sejcf,jfd->sejcd/dot_general | solution.py:91
  190.9 5.9 %copy.25 = bf16[8,8,2,12,1280]{4,1,3,2,0:T(8,128)(2,1)} copy(bf16[8,8,2,12,1280]{4,3,1,0,2:T(8,128)(2,1)} %fusion.22) | data formatting | bytes 7864320 | tf_op jit(solution)/shard_map/convert_element_type | solution.py:93
  196.8 0.0 reduce-scatter.2.cloned.1.call-update
  196.9 51.6 %reduce-scatter.2.cloned.1.call-done = bf16[1,8,2,12,1280]{4,1,3,2,0:T(8,128)(2,1)} async-done(((bf16[8,8,2,12,1280]{4,1,3,2,0:T(8,128)(2,1)}), bf16[1,8,2,12,1280]{4,1,3,2,0:T(8,128)(2,1)}) %reduce-scatter.2.cloned.1.call-update) | async-done | bytes 491536 | tf_op jit(solution)/shard_map/reduce_scatter | solution.py:94
  248.5 1.5 copy.26
  250.0 16.5 %all_to_all.44 = bf16[8,2,12,1280]{3,1,2,0:T(2,128)(2,1)S(1)} all-to-all(bf16[8,2,12,1280]{3,1,2,0:T(2,128)(2,1)S(1)} %copy.26), channel_id=1, replica_groups=mesh['seq'=8,'exp'=8,'img'=4] {'exp'}, dimensions={0} | all-to-all | bytes 983040 | tf_op jit(solution)/shard_map/all_to_all | solution.py:95
  266.5 0.9 copy.27
  267.4 2.0 reshape.42
  269.4 2.3 fusion.48
  (2 shorter events, 0.0 us)
Async XLA Ops:
  6.5 162.3 %copy-start = (bf16[2,640,1280]{2,1,0:T(8,128)(2,1)S(1)}, bf16[2,640,1280]{2,1,0:T(8,128)(2,1)}, u32[]{:S(2)}) copy-start(bf16[2,640,1280]{2,1,0:T(8,128)(2,1)} %param.15) | copy-start | bytes 9830404
  6.5 86.7 %all-gather.4.cloned.1.call-start = ((), (), s32[]{:S(2)}) async-start(), calls=%async_computation.5 | async-start | bytes 3686400 | tf_op jit(solution)/shard_map/all_gather | solution.py:65
  12.0 46.4 %all-to-all-start = ((bf16[128,3,8,2,80]{0,4,3,1,2:T(8,128)(2,1)}), bf16[128,3,8,2,80]{0,4,3,1,2:T(8,128)(2,1)}, u32[]{:S(2)}, u32[]{:S(2)}) async-start(bf16[128,3,8,2,80]{0,4,3,1,2:T(8,128)(2,1)} %copy.19), calls=%async_computation | async-start | bytes 1966080 | tf_op jit(solution)/shard_map/all_to_all | solution.py:58
  74.8 22.1 %copy-start.2 = (f32[1280]{0:T(1024)S(1)}, f32[1280]{0:T(1024)}, u32[]{:S(2)}) copy-start(f32[1280]{0:T(1024)} %param.12) | copy-start | bytes 15364
  74.8 22.1 %copy-start.3 = (f32[1280]{0:T(1024)S(1)}, f32[1280]{0:T(1024)}, u32[]{:S(2)}) copy-start(f32[1280]{0:T(1024)} %param.11) | copy-start | bytes 15364
  75.6 17.6 %all-to-all-start.1 = ((bf16[8,128,1,160]{1,3,2,0:T(8,128)(2,1)}), bf16[8,128,1,160]{1,3,2,0:T(8,128)(2,1)}, u32[]{:S(2)}, u32[]{:S(2)}) async-start(bf16[8,128,1,160]{1,3,2,0:T(8,128)(2,1)} %copy.22), calls=%async_computation.1 | async-start | bytes 655360 | tf_op jit(solution)/shard_map/all_to_all | solution.py:60
  79.7 83.9 %all-gather.6.cloned.1.call-start = ((), (), s32[]{:S(2)}) async-start(), calls=%async_computation.7 | async-start | bytes 4423680 | tf_op jit(solution)/shard_map/all_gather | solution.py:86
  96.0 0.9 copy-start.1
  118.0 130.5 %reduce-scatter.2.cloned.1.call-start = ((), (), s32[]{:S(2)}) async-start(), calls=%async_computation.6 | async-start | bytes 4423680 | tf_op jit(solution)/shard_map/reduce_scatter | solution.py:94
Sparse Core Ops, SparseCore 0:
  9.1 67.2 all-gather.3
  118.1 45.5 all-gather.5
  197.0 51.4 reduce-scatter.1
where the time goes:
time: 279 us; the launch traced here: 278 us
  waiting for transfers between devices  147 us (53%)
  matrix products  39.8 us (14%)
  blocking collectives  32.9 us (12%)
  local copies, waits for them, and re-layouts  30.6 us (11%)
  between operations  13.2 us (5%)
  starting transfers between devices  12.8 us (5%)
    reduce_scatter x1, waiting for transfers between devices, per_device(): summed = lax.psum_scatter(pieces, 'seq', scatter_dimension=0, tiled=True)[0]  51.6 us
    all_gather x1, waiting for transfers between devices, per_device(): gathered = lax.all_gather(arrived, 'seq', axis=0, tiled=False)  45.5 us
    all_to_all x1, waiting for transfers between devices, per_device(): lax.all_to_all(regrouped, 'seq', split_axis=2, concat_axis=0, tiled=True)  38 us
    dot_general x1, matrix products, per_device(): jnp.einsum('sejcf,jfd->sejcd', hidden, expert_down, preferred_element_typ...  22.1 us
    all_to_all x1, blocking collectives, per_device(): lax.all_to_all(summed, 'exp', split_axis=0, concat_axis=0, tiled=True)  16.5 us
    all_to_all x1, blocking collectives, per_device(): lax.all_to_all(dispatch, 'exp', split_axis=0, concat_axis=0, tiled=True)  16.4 us
    all_to_all x1, waiting for transfers between devices, per_device(): lax.all_to_all(attended, 'seq', split_axis=0, concat_axis=2, tiled=True)  11.7 us
    all_to_all x1, starting transfers between devices, per_device(): lax.all_to_all(regrouped, 'seq', split_axis=2, concat_axis=0, tiled=True)  8.47 us
  transfers between devices with their start and end apart: 5, of which 4 were waited for; matrix products, arithmetic and copies ran while one was open for 8% of the time, Pallas kernels for 0%

commit v1 on v0

--- a/solution.py
+++ b/solution.py
@@ -8,28 +8,19 @@
 
 
 def attend(gathered):
-    queries = gathered[:, 0, 0]
-    keys_all = gathered[:, 1, 0]
-    values = gathered[:, 2, 0]
-    length = queries.shape[0]
-    span_rows = length
+    queries = gathered[0]
+    keys_all = gathered[1]
+    values = gathered[2]
     factor = 1.0 / queries.shape[2] ** 0.5
-
-    def one_block(offset):
-        query_rows = lax.dynamic_slice_in_dim(queries, offset, span_rows, 0)
-        scores = (
-            jnp.einsum("qhd,khd->hqk", query_rows, keys_all, preferred_element_type=jnp.float32)
-            * factor
-        )
-        peak = jnp.max(scores, axis=-1, keepdims=True)
-        powers = jnp.exp(scores - peak)
-        weights = (powers / jnp.sum(powers, axis=-1, keepdims=True)).astype(jnp.bfloat16)
-        mixed = jnp.einsum("hqk,khd->qhd", weights, values, preferred_element_type=jnp.float32)
-        return mixed.astype(jnp.bfloat16)
-
-    starts = jnp.arange(length // span_rows, dtype=jnp.int32) * span_rows
-    blocks = lax.map(one_block, starts)
-    return blocks.reshape(length, queries.shape[1], queries.shape[2])
+    scores = (
+        jnp.einsum("ahdb,chde->habce", queries, keys_all, preferred_element_type=jnp.float32)
+        * factor
+    )
+    peak = jnp.max(scores, axis=(3, 4), keepdims=True)
+    powers = jnp.exp(scores - peak)
+    weights = (powers / jnp.sum(powers, axis=(3, 4), keepdims=True)).astype(jnp.bfloat16)
+    mixed = jnp.einsum("habce,chde->abhd", weights, values, preferred_element_type=jnp.float32)
+    return mixed.astype(jnp.bfloat16)
 
 
 def layer_norm(stream, norm_gain, norm_bias):
@@ -54,8 +45,11 @@
     length = tok_rows * seq_count
     heads_here = HEADS // seq_count
     head_width = heads_here * HEAD_DIM
-    regrouped = projected[0].reshape(tok_rows, 3, seq_count, heads_here, HEAD_DIM)
-    attended = attend(lax.all_to_all(regrouped, "seq", split_axis=2, concat_axis=0, tiled=True))
+    token_minor = jnp.transpose(projected[0], (1, 2, 0)).reshape(
+        3, seq_count, head_width, tok_rows
+    )
+    arrived_heads = lax.all_to_all(token_minor, "seq", split_axis=1, concat_axis=1, tiled=True)
+    attended = attend(arrived_heads.reshape(3, seq_count, heads_here, HEAD_DIM, tok_rows))
     attended = attended.reshape(seq_count, tok_rows, 1, head_width)
     token_heads = lax.all_to_all(attended, "seq", split_axis=0, concat_axis=2, tiled=True).reshape(
         tok_rows, model_width

time: 279 us -> 272 us (0.975)
  matrix products: 39.8 us -> 31.6 us
  local copies, waits for them, and re-layouts: 30.6 us -> 27 us
  waiting for transfers between devices: 147 us -> 150 us
    sub x1 -> x0, matrix products: 7.07 us -> none  [one_block(): powers = jnp.exp(scores - peak)]
    all_to_all x2 -> x0, local copies, waits for them, and re-layouts: 4.85 us -> none  [per_device(): lax.all_to_all(regrouped, 'seq', split_axis=2, concat_axis=0, tiled=True)]
    another operation x2 -> x0, local copies, waits for them, and re-layouts: 3.02 us -> none  [the longest x1 2.25 us: per_device(): projected[0].reshape(tok_rows, 3, seq_count, heads_here, HEAD_DIM)]
    all_to_all x1, waiting for transfers between devices: 11.7 us -> 14.6 us  [per_device(): lax.all_to_all(attended, 'seq', split_axis=0, concat_axis=2, tiled=True)]
  transfers between devices with their start and end apart: 5 -> 5, of which waited for: 4 -> 4; matrix products, arithmetic and copies ran while one was open for 8% -> 5% of each run, Pallas kernels for 0% -> 0%
where the time goes in v1:
time: 272 us; the launch traced here: 271 us
  waiting for transfers between devices  150 us (55%)
  blocking collectives  33.4 us (12%)
  matrix products  31.6 us (12%)
  local copies, waits for them, and re-layouts  27 us (10%)
  between operations  13.2 us (5%)
  starting transfers between devices  12.8 us (5%)
    reduce_scatter x1, waiting for transfers between devices, per_device(): summed = lax.psum_scatter(pieces, 'seq', scatter_dimension=0, tiled=True)[0]  51.6 us
    all_gather x1, waiting for transfers between devices, per_device(): gathered = lax.all_gather(arrived, 'seq', axis=0, tiled=False)  45.5 us
    all_to_all x1, waiting for transfers between devices, per_device(): lax.all_to_all(token_minor, 'seq', split_axis=1, concat_axis=1, tiled=True)  38 us
    dot_general x1, matrix products, per_device(): jnp.einsum('sejcf,jfd->sejcd', hidden, expert_down, preferred_element_typ...  22.1 us
    all_to_all x1, blocking collectives, per_device(): lax.all_to_all(dispatch, 'exp', split_axis=0, concat_axis=0, tiled=True)  16.9 us
    all_to_all x1, blocking collectives, per_device(): lax.all_to_all(summed, 'exp', split_axis=0, concat_axis=0, tiled=True)  16.5 us
    all_to_all x1, waiting for transfers between devices, per_device(): lax.all_to_all(attended, 'seq', split_axis=0, concat_axis=2, tiled=True)  14.6 us
    all_to_all x1, starting transfers between devices, per_device(): lax.all_to_all(token_minor, 'seq', split_axis=1, concat_axis=1, tiled=True)  8.47 us
  transfers between devices with their start and end apart: 5, of which 4 were waited for; matrix products, arithmetic and copies ran while one was open for 5% of the time, Pallas kernels for 0%

profile of v1, /device:TPU:8, one launch (start us, length us, event | category | flops | bytes accessed | tf_op | source)
XLA Modules:
  0.0 271.1 jit_solution(11405088259378467511)
XLA Ops:
  6.5 0.0 copy-start
  6.5 0.0 all-gather.4.cloned.1.call-start
  6.5 0.7 all-gather.4.cloned.1.call-update
  7.3 2.5 copy.19
  9.8 2.2 copy.20
  12.0 8.5 %all-to-all-start = ((bf16[3,8,160,128]{3,2,0,1:T(8,128)(2,1)}), bf16[3,8,160,128]{3,2,0,1:T(8,128)(2,1)}, u32[]{:S(2)}, u32[]{:S(2)}) async-start(bf16[3,8,160,128]{3,2,0,1:T(8,128)(2,1)} %copy.20), calls=%async_computation | async-start | bytes 1966080 | tf_op jit(solution)/shard_map/all_to_all | solution.py:51
  20.5 38.0 %all-to-all-done = bf16[3,8,160,128]{3,2,0,1:T(8,128)(2,1)} async-done(((bf16[3,8,160,128]{3,2,0,1:T(8,128)(2,1)}), bf16[3,8,160,128]{3,2,0,1:T(8,128)(2,1)}, u32[]{:S(2)}, u32[]{:S(2)}) %all-to-all-start) | async-done | bytes 983072 | tf_op jit(solution)/shard_map/all_to_all | solution.py:51
  58.4 1.2 fusion.86
  59.7 1.3 multiply_reduce_fusion
  61.0 1.4 fusion
  62.4 2.0 fusion.47
  64.3 0.0 copy-start.2
  64.4 0.0 copy-start.3
  64.4 0.7 copy.28
  65.1 4.1 %all-to-all-start.1 = ((bf16[8,128,1,160]{1,3,2,0:T(8,128)(2,1)}), bf16[8,128,1,160]{1,3,2,0:T(8,128)(2,1)}, u32[]{:S(2)}, u32[]{:S(2)}) async-start(bf16[8,128,1,160]{1,3,2,0:T(8,128)(2,1)} %bitcast.135), calls=%async_computation.1 | async-start | bytes 655360 | tf_op jit(solution)/shard_map/all_to_all | solution.py:54
  69.2 0.0 all-gather.6.cloned.1.call-start
  69.3 0.7 dynamic-slice_bitcast_fusion
  69.9 0.1 fusion.54
  70.0 0.2 reduce_window_sum.11
  70.2 0.2 select_reduce_fusion
  70.4 0.7 multiply_add_fusion
  71.0 14.6 %all-to-all-done.1 = bf16[8,128,1,160]{1,3,2,0:T(8,128)(2,1)} async-done(((bf16[8,128,1,160]{1,3,2,0:T(8,128)(2,1)}), bf16[8,128,1,160]{1,3,2,0:T(8,128)(2,1)}, u32[]{:S(2)}, u32[]{:S(2)}) %all-to-all-start.1) | async-done | bytes 327712 | tf_op jit(solution)/shard_map/all_to_all | solution.py:54
  85.6 0.0 all-gather.4.cloned.1.call-done
  85.6 2.8 %fusion.87 = (f32[128]{0:T(128)S(1)}, f32[128,1280]{1,0:T(8,128)S(1)}) fusion(bf16[128,1280]{0,1:T(8,128)(2,1)} %bitcast.16, bf16[1280,1280]{1,0:T(8,128)(2,1)} %all-gather.4.cloned.1.call-done, bf16[1,128,1280]{2,1,0:T(8,128)(2,1)} %param.9), kind=kOutput, calls=%fused_computation.107 | convolution fusion | flops 420249472 | bytes 4588032 | tf_op jit(solution)/shard_map/dot_general | solution.py:57
  88.4 0.0 copy-start.1
  88.4 0.2 multiply_reduce_fusion.1
  88.7 0.6 copy-done.1
  89.3 0.0 copy-done.2
  89.3 0.0 copy-done.3
  89.3 1.2 convolution_convert_fusion.1
  90.5 2.0 reshape.55
  92.5 1.5 copy.29
  93.9 16.9 %all_to_all.30 = bf16[8,2,12,1280]{3,1,2,0:T(2,128)(2,1)} all-to-all(bf16[8,2,12,1280]{3,1,2,0:T(2,128)(2,1)S(1)} %copy.29), channel_id=1, replica_groups=mesh['seq'=8,'exp'=8,'img'=4] {'exp'}, dimensions={0} | all-to-all | bytes 983040 | tf_op jit(solution)/shard_map/all_to_all | solution.py:79
  110.9 0.0 all-gather.6.cloned.1.call-update
  110.9 0.2 reduce-scatter.2.cloned.1.call-start
  111.1 45.5 %all-gather.6.cloned.1.call-done = bf16[64,2,12,1280]{3,1,2,0:T(2,128)(2,1)} async-done(((bf16[8,2,12,1280]{3,1,2,0:T(2,128)(2,1)}), bf16[64,2,12,1280]{3,1,2,0:T(2,128)(2,1)}) %all-gather.6.cloned.1.call-update) | async-done | bytes 3932176 | tf_op jit(solution)/shard_map/all_gather | solution.py:80
  156.6 5.2 %copy.30 = bf16[64,2,12,1280]{3,2,0,1:T(8,128)(2,1)} copy(bf16[64,2,12,1280]{3,1,2,0:T(2,128)(2,1)} %all-gather.6.cloned.1.call-done) | data formatting | bytes 7864320 | tf_op jit(solution)/shard_map/all_gather | solution.py:80
  161.7 0.0 copy-done
  161.7 22.1 %fusion.19 = bf16[8,8,2,12,1280]{4,3,1,0,2:T(8,128)(2,1)} fusion(bf16[2,640,1280]{2,1,0:T(8,128)(2,1)S(1)} %copy-done, bf16[8,8,2,12,1280]{4,3,1,0,2:T(8,128)(2,1)} %bitcast.131, bf16[2,1280,640]{2,1,0:T(8,128)(2,1)} %param.14), kind=kOutput, calls=%fused_computation.29 | convolution fusion | flops 5099028480 | bytes 14417920 | tf_op jit(solution)/shard_map/sejcf,jfd->sejcd/dot_general | solution.py:85
  183.9 5.9 %copy.31 = bf16[8,8,2,12,1280]{4,1,3,2,0:T(8,128)(2,1)} copy(bf16[8,8,2,12,1280]{4,3,1,0,2:T(8,128)(2,1)} %fusion.19) | data formatting | bytes 7864320 | tf_op jit(solution)/shard_map/convert_element_type | solution.py:87
  189.8 0.0 reduce-scatter.2.cloned.1.call-update
  189.8 51.6 %reduce-scatter.2.cloned.1.call-done = bf16[1,8,2,12,1280]{4,1,3,2,0:T(8,128)(2,1)} async-done(((bf16[8,8,2,12,1280]{4,1,3,2,0:T(8,128)(2,1)}), bf16[1,8,2,12,1280]{4,1,3,2,0:T(8,128)(2,1)}) %reduce-scatter.2.cloned.1.call-update) | async-done | bytes 491536 | tf_op jit(solution)/shard_map/reduce_scatter | solution.py:88
  241.4 1.5 copy.32
  242.9 16.5 %all_to_all.31 = bf16[8,2,12,1280]{3,1,2,0:T(2,128)(2,1)S(1)} all-to-all(bf16[8,2,12,1280]{3,1,2,0:T(2,128)(2,1)S(1)} %copy.32), channel_id=1, replica_groups=mesh['seq'=8,'exp'=8,'img'=4] {'exp'}, dimensions={0} | all-to-all | bytes 983040 | tf_op jit(solution)/shard_map/all_to_all | solution.py:89
  259.4 0.9 copy.33
  260.3 2.0 reshape.56
  262.3 2.3 fusion.44
  (2 shorter events, 0.0 us)
Async XLA Ops:
  6.5 155.2 %copy-start = (bf16[2,640,1280]{2,1,0:T(8,128)(2,1)S(1)}, bf16[2,640,1280]{2,1,0:T(8,128)(2,1)}, u32[]{:S(2)}) copy-start(bf16[2,640,1280]{2,1,0:T(8,128)(2,1)} %param.15) | copy-start | bytes 9830404
  6.5 79.1 %all-gather.4.cloned.1.call-start = ((), (), s32[]{:S(2)}) async-start(), calls=%async_computation.5 | async-start | bytes 3686400 | tf_op jit(solution)/shard_map/all_gather | solution.py:59
  12.0 46.4 %all-to-all-start = ((bf16[3,8,160,128]{3,2,0,1:T(8,128)(2,1)}), bf16[3,8,160,128]{3,2,0,1:T(8,128)(2,1)}, u32[]{:S(2)}, u32[]{:S(2)}) async-start(bf16[3,8,160,128]{3,2,0,1:T(8,128)(2,1)} %copy.20), calls=%async_computation | async-start | bytes 1966080 | tf_op jit(solution)/shard_map/all_to_all | solution.py:51
  64.3 25.0 %copy-start.2 = (f32[1280]{0:T(1024)S(1)}, f32[1280]{0:T(1024)}, u32[]{:S(2)}) copy-start(f32[1280]{0:T(1024)} %param.12) | copy-start | bytes 15364
  64.4 24.9 %copy-start.3 = (f32[1280]{0:T(1024)S(1)}, f32[1280]{0:T(1024)}, u32[]{:S(2)}) copy-start(f32[1280]{0:T(1024)} %param.11) | copy-start | bytes 15364
  65.1 20.5 %all-to-all-start.1 = ((bf16[8,128,1,160]{1,3,2,0:T(8,128)(2,1)}), bf16[8,128,1,160]{1,3,2,0:T(8,128)(2,1)}, u32[]{:S(2)}, u32[]{:S(2)}) async-start(bf16[8,128,1,160]{1,3,2,0:T(8,128)(2,1)} %bitcast.135), calls=%async_computation.1 | async-start | bytes 655360 | tf_op jit(solution)/shard_map/all_to_all | solution.py:54
  69.2 87.4 %all-gather.6.cloned.1.call-start = ((), (), s32[]{:S(2)}) async-start(), calls=%async_computation.7 | async-start | bytes 4423680 | tf_op jit(solution)/shard_map/all_gather | solution.py:80
  88.4 0.9 copy-start.1
  110.9 130.5 %reduce-scatter.2.cloned.1.call-start = ((), (), s32[]{:S(2)}) async-start(), calls=%async_computation.6 | async-start | bytes 4423680 | tf_op jit(solution)/shard_map/reduce_scatter | solution.py:88
Sparse Core Ops, SparseCore 0:
  9.1 72.3 all-gather.3
  111.0 45.5 all-gather.5
  189.9 51.4 reduce-scatter.1

commit v2 on v1

--- a/solution.py
+++ b/solution.py
@@ -78,13 +78,22 @@
     dispatch = dispatch.reshape(exp_count, local_experts, cap_dev, model_width)
     arrived = lax.all_to_all(dispatch, "exp", split_axis=0, concat_axis=0, tiled=True)
     gathered = lax.all_gather(arrived, "seq", axis=0, tiled=False)
-    hidden = jax.nn.gelu(
-        jnp.einsum("sejcd,jdf->sejcf", gathered, expert_up, preferred_element_type=jnp.float32),
-        approximate=False,
-    ).astype(jnp.bfloat16)
-    pieces = jnp.einsum(
-        "sejcf,jfd->sejcd", hidden, expert_down, preferred_element_type=jnp.float32
-    ).astype(jnp.bfloat16)
+    pieces = []
+    for local in range(local_experts):
+        hidden = jax.nn.gelu(
+            jnp.einsum(
+                "secd,df->secf",
+                gathered[:, :, local],
+                expert_up[local],
+                preferred_element_type=jnp.float32,
+            ),
+            approximate=False,
+        ).astype(jnp.bfloat16)
+        piece = jnp.einsum(
+            "secf,fd->secd", hidden, expert_down[local], preferred_element_type=jnp.float32
+        )
+        pieces.append(piece.astype(jnp.bfloat16))
+    pieces = jnp.stack(pieces, axis=2)
     summed = lax.psum_scatter(pieces, "seq", scatter_dimension=0, tiled=True)[0]
     returned = lax.all_to_all(summed, "exp", split_axis=0, concat_axis=0, tiled=True).reshape(
         experts * cap_dev, model_width

time: 272 us -> 257 us (0.945)
  local copies, waits for them, and re-layouts: 27 us -> 12.8 us
  waiting for transfers between devices: 150 us -> 154 us
  matrix products: 31.6 us -> 28.8 us
    convert_element_type x1 -> x0, local copies, waits for them, and re-layouts: 5.9 us -> none  [per_device(): pieces = jnp.einsum('sejcf,jfd->sejcd', hidden, expert_down, preferred_el...]
    another operation x0 -> x1, local copies, waits for them, and re-layouts: none -> 3.4 us  [per_device(): pieces = jnp.stack(pieces, axis=2)]
    all_gather x1, waiting for transfers between devices: 45.5 us -> 48.8 us  [per_device(): gathered = lax.all_gather(arrived, 'seq', axis=0, tiled=False)]
    reshape x2, local copies, waits for them, and re-layouts: 3.44 us -> 0.49 us  [per_device(): dispatch = dispatch.reshape(exp_count, local_experts, cap_dev, model_width)]
    dot_general x1 -> x4, matrix products: 22.1 us -> 21.4 us  [the longest x2 16.1 us: per_device(): jnp.einsum('secf,fd->secd', hidden, expert_down[local], preferred_element...]
  transfers between devices with their start and end apart: 5 -> 5, of which waited for: 4 -> 4; matrix products, arithmetic and copies ran while one was open for 5% -> 4% of each run, Pallas kernels for 0% -> 0%
where the time goes in v2:
time: 257 us
  waiting for transfers between devices  154 us (60%)
  blocking collectives  32.8 us (13%)
  matrix products  28.8 us (11%)
  between operations  13.3 us (5%)
  local copies, waits for them, and re-layouts  12.8 us (5%)
  starting transfers between devices  12 us (5%)
  other arithmetic  3.41 us (1%)
    reduce_scatter x1, waiting for transfers between devices, per_device(): summed = lax.psum_scatter(pieces, 'seq', scatter_dimension=0, tiled=True)[0]  51.6 us
    all_gather x1, waiting for transfers between devices, per_device(): gathered = lax.all_gather(arrived, 'seq', axis=0, tiled=False)  48.8 us
    all_to_all x1, waiting for transfers between devices, per_device(): lax.all_to_all(token_minor, 'seq', split_axis=1, concat_axis=1, tiled=True)  36.7 us
    all_to_all x1, blocking collectives, per_device(): lax.all_to_all(summed, 'exp', split_axis=0, concat_axis=0, tiled=True)  16.5 us
    all_to_all x1, blocking collectives, per_device(): lax.all_to_all(dispatch, 'exp', split_axis=0, concat_axis=0, tiled=True)  16.3 us
    dot_general x2, matrix products, per_device(): jnp.einsum('secf,fd->secd', hidden, expert_down[local], preferred_element...  16.1 us
    all_to_all x1, waiting for transfers between devices, per_device(): lax.all_to_all(attended, 'seq', split_axis=0, concat_axis=2, tiled=True)  15.7 us
    all_to_all x1, starting transfers between devices, per_device(): lax.all_to_all(token_minor, 'seq', split_axis=1, concat_axis=1, tiled=True)  8.47 us
  transfers between devices with their start and end apart: 5, of which 4 were waited for; matrix products, arithmetic and copies ran while one was open for 4% of the time, Pallas kernels for 0%

profile of v2, /device:TPU:8, one launch (start us, length us, event | category | flops | bytes accessed | tf_op | source)
XLA Modules:
  0.0 256.7 jit_solution(7431456317429387163)
XLA Ops:
  6.5 0.0 all-gather.4.cloned.1.call-start
  6.5 0.7 all-gather.4.cloned.1.call-update
  7.3 1.6 copy.19
  8.9 1.0 copy.20
  9.9 8.5 %all-to-all-start = ((bf16[3,8,160,128]{3,2,0,1:T(8,128)(2,1)}), bf16[3,8,160,128]{3,2,0,1:T(8,128)(2,1)S(1)}, u32[]{:S(2)}, u32[]{:S(2)}) async-start(bf16[3,8,160,128]{3,2,0,1:T(8,128)(2,1)} %copy.20), calls=%async_computation | async-start | bytes 1966080 | tf_op jit(solution)/shard_map/all_to_all | solution.py:51
  18.4 36.7 %all-to-all-done = bf16[3,8,160,128]{3,2,0,1:T(8,128)(2,1)S(1)} async-done(((bf16[3,8,160,128]{3,2,0,1:T(8,128)(2,1)}), bf16[3,8,160,128]{3,2,0,1:T(8,128)(2,1)S(1)}, u32[]{:S(2)}, u32[]{:S(2)}) %all-to-all-start) | async-done | bytes 983072 | tf_op jit(solution)/shard_map/all_to_all | solution.py:51
  55.1 0.1 fusion.181
  55.2 1.3 multiply_reduce_fusion
  56.5 1.4 fusion
  57.8 0.0 copy-start
  57.9 2.0 fusion.102
  59.9 0.7 copy.28
  60.6 3.4 %all-to-all-start.1 = ((bf16[8,128,1,160]{1,3,2,0:T(8,128)(2,1)}), bf16[8,128,1,160]{1,3,2,0:T(8,128)(2,1)S(1)}, u32[]{:S(2)}, u32[]{:S(2)}) async-start(bf16[8,128,1,160]{1,3,2,0:T(8,128)(2,1)} %bitcast.13), calls=%async_computation.1 | async-start | bytes 655360 | tf_op jit(solution)/shard_map/all_to_all | solution.py:54
  64.0 0.0 all-gather.6.cloned.1.call-start
  64.1 0.7 dynamic-slice_bitcast_fusion
  64.8 0.1 fusion.117
  64.8 0.2 reduce_window_sum.11
  65.0 0.2 select_reduce_fusion
  65.2 0.7 multiply_add_fusion
  65.9 15.7 %all-to-all-done.1 = bf16[8,128,1,160]{1,3,2,0:T(8,128)(2,1)S(1)} async-done(((bf16[8,128,1,160]{1,3,2,0:T(8,128)(2,1)}), bf16[8,128,1,160]{1,3,2,0:T(8,128)(2,1)S(1)}, u32[]{:S(2)}, u32[]{:S(2)}) %all-to-all-start.1) | async-done | bytes 327712 | tf_op jit(solution)/shard_map/all_to_all | solution.py:54
  81.6 0.0 copy-done
  81.6 2.7 %fusion.182 = (f32[128]{0:T(128)S(1)}, f32[128,1280]{1,0:T(8,128)S(1)}) fusion(bf16[128,1280]{0,1:T(8,128)(2,1)S(1)} %bitcast.98, bf16[1280,1280]{1,0:T(8,128)(2,1)} %all-gather.4.cloned.1.call-done, bf16[1,128,1280]{2,1,0:T(8,128)(2,1)S(1)} %copy-done), kind=kOutput, calls=%fused_computation.225 | convolution fusion | flops 420249472 | bytes 4588032 | tf_op jit(solution)/shard_map/dot_general | solution.py:57
  84.3 0.2 multiply_reduce_fusion.1
  84.5 0.0 copy-done.3
  84.6 0.4 convolution_convert_fusion.2
  85.0 0.1 reshape.55
  85.1 0.4 copy.29
  85.5 16.3 %all_to_all.30 = bf16[8,2,12,1280]{3,1,2,0:T(2,128)(2,1)} all-to-all(bf16[8,2,12,1280]{3,1,2,0:T(2,128)(2,1)S(1)} %copy.29), channel_id=1, replica_groups=mesh['seq'=8,'exp'=8,'img'=4] {'exp'}, dimensions={0} | all-to-all | bytes 983040 | tf_op jit(solution)/shard_map/all_to_all | solution.py:79
  101.8 0.0 all-gather.6.cloned.1.call-update
  101.8 0.0 reduce-scatter.2.cloned.1.call-start
  101.9 48.8 %all-gather.6.cloned.1.call-done = bf16[64,2,12,1280]{3,1,2,0:T(2,128)(2,1)} async-done(((bf16[8,2,12,1280]{3,1,2,0:T(2,128)(2,1)}), bf16[64,2,12,1280]{3,1,2,0:T(2,128)(2,1)}) %all-gather.6.cloned.1.call-update) | async-done | bytes 3932176 | tf_op jit(solution)/shard_map/all_gather | solution.py:80
  150.7 3.0 %copy.30 = bf16[64,2,12,1280]{3,2,0,1:T(8,128)(2,1)S(1)} copy(bf16[64,2,12,1280]{3,1,2,0:T(2,128)(2,1)} %all-gather.6.cloned.1.call-done) | data formatting | bytes 7864320 | tf_op jit(solution)/shard_map/all_gather | solution.py:80
  153.7 0.1 copy-done.1
  153.8 2.6 %fusion.105 = (u8[8,12,640]{2,1,0:T(8,128)(4,1)S(1)}, u8[8,12,640]{2,1,0:T(8,128)(4,1)S(1)}, f32[8,8,12,640]{3,2,1,0:T(8,128)S(1)}) fusion(bf16[2,1280,640]{2,1,0:T(8,128)(2,1)S(1)} %copy-done.1, bf16[8,8,2,12,1280]{4,3,1,0,2:T(8,128)(2,1)S(1)} %bitcast.95), kind=kOutput, calls=%fused_computation.141 | convolution fusion | flops 1264558080 | bytes 6348800 | tf_op jit(solution)/shard_map/secd,df->secf/dot_general | solution.py:84
  156.4 0.0 copy-start.2
  156.4 2.6 %fusion.106 = (u8[8,12,640]{2,1,0:T(8,128)(4,1)S(1)}, u8[8,12,640]{2,1,0:T(8,128)(4,1)S(1)}, f32[8,8,12,640]{3,2,1,0:T(8,128)S(1)}) fusion(bf16[2,1280,640]{2,1,0:T(8,128)(2,1)S(1)} %copy-done.1, bf16[8,8,2,12,1280]{4,3,1,0,2:T(8,128)(2,1)S(1)} %bitcast.96), kind=kOutput, calls=%fused_computation.142 | convolution fusion | flops 1264558080 | bytes 6348800 | tf_op jit(solution)/shard_map/secd,df->secf/dot_general | solution.py:84
  159.0 0.0 copy-done.2
  159.0 8.2 %fusion.2 = bf16[8,8,1,12,1280]{4,3,1,0,2:T(8,128)(2,1)S(1)} fusion(bf16[2,640,1280]{2,1,0:T(8,128)(2,1)S(1)} %copy-done.2, f32[8,8,12,640]{3,2,1,0:T(8,128)S(1)} %get-tuple-element.17, u8[8,12,640]{2,1,0:T(8,128)(4,1)S(1)} %get-tuple-element.6, u8[8,12,640]{2,1,0:T(8,128)(4,1)S(1)} %get-tuple-element.5), kind=kOutput, calls=%fused_computation.10 | convolution fusion | flops 1293680640 | bytes 6389760 | tf_op jit(solution)/shard_map/secf,fd->secd/dot_general | solution.py:92
  167.2 8.0 %fusion.3 = bf16[8,8,1,12,1280]{4,3,1,0,2:T(8,128)(2,1)S(1)} fusion(bf16[2,640,1280]{2,1,0:T(8,128)(2,1)S(1)} %copy-done.2, f32[8,8,12,640]{3,2,1,0:T(8,128)S(1)} %get-tuple-element.16, u8[8,12,640]{2,1,0:T(8,128)(4,1)S(1)} %get-tuple-element.8, u8[8,12,640]{2,1,0:T(8,128)(4,1)S(1)} %get-tuple-element.7), kind=kOutput, calls=%fused_computation.11 | convolution fusion | flops 1293680640 | bytes 6389760 | tf_op jit(solution)/shard_map/secf,fd->secd/dot_general | solution.py:92
  175.2 0.7 pad_maximum_fusion
  175.9 3.4 %copy.31 = bf16[8,8,2,12,1280]{4,1,3,2,0:T(8,128)(2,1)} copy(bf16[8,8,2,12,1280]{4,3,1,0,2:T(8,128)(2,1)S(1)} %pad_maximum_fusion) | data formatting | bytes 7864320 | tf_op jit(solution)/shard_map/stack | solution.py:96
  179.3 0.0 reduce-scatter.2.cloned.1.call-update
  179.3 51.6 %reduce-scatter.2.cloned.1.call-done = bf16[1,8,2,12,1280]{4,1,3,2,0:T(8,128)(2,1)} async-done(((bf16[8,8,2,12,1280]{4,1,3,2,0:T(8,128)(2,1)}), bf16[1,8,2,12,1280]{4,1,3,2,0:T(8,128)(2,1)}) %reduce-scatter.2.cloned.1.call-update) | async-done | bytes 491536 | tf_op jit(solution)/shard_map/reduce_scatter | solution.py:97
  230.9 1.5 copy.32
  232.5 16.5 %all_to_all.31 = bf16[8,2,12,1280]{3,1,2,0:T(2,128)(2,1)S(1)} all-to-all(bf16[8,2,12,1280]{3,1,2,0:T(2,128)(2,1)S(1)} %copy.32), channel_id=1, replica_groups=mesh['seq'=8,'exp'=8,'img'=4] {'exp'}, dimensions={0} | all-to-all | bytes 983040 | tf_op jit(solution)/shard_map/all_to_all | solution.py:98
  249.0 0.1 copy.33
  249.0 0.1 reshape.56
  249.1 1.0 fusion.27
  (7 shorter events, 0.0 us)
Async XLA Ops:
  6.5 75.1 %all-gather.4.cloned.1.call-start = ((), (), s32[]{:S(2)}) async-start(), calls=%async_computation.5 | async-start | bytes 3686400 | tf_op jit(solution)/shard_map/all_gather | solution.py:59
  9.9 45.2 %all-to-all-start = ((bf16[3,8,160,128]{3,2,0,1:T(8,128)(2,1)}), bf16[3,8,160,128]{3,2,0,1:T(8,128)(2,1)S(1)}, u32[]{:S(2)}, u32[]{:S(2)}) async-start(bf16[3,8,160,128]{3,2,0,1:T(8,128)(2,1)} %copy.20), calls=%async_computation | async-start | bytes 1966080 | tf_op jit(solution)/shard_map/all_to_all | solution.py:51
  57.8 23.8 %copy-start = (bf16[1,128,1280]{2,1,0:T(8,128)(2,1)S(1)}, bf16[1,128,1280]{2,1,0:T(8,128)(2,1)}, u32[]{:S(2)}) copy-start(bf16[1,128,1280]{2,1,0:T(8,128)(2,1)} %param.9) | copy-start | bytes 983044
  60.6 21.0 %all-to-all-start.1 = ((bf16[8,128,1,160]{1,3,2,0:T(8,128)(2,1)}), bf16[8,128,1,160]{1,3,2,0:T(8,128)(2,1)S(1)}, u32[]{:S(2)}, u32[]{:S(2)}) async-start(bf16[8,128,1,160]{1,3,2,0:T(8,128)(2,1)} %bitcast.13), calls=%async_computation.1 | async-start | bytes 655360 | tf_op jit(solution)/shard_map/all_to_all | solution.py:54
  64.0 86.6 %all-gather.6.cloned.1.call-start = ((), (), s32[]{:S(2)}) async-start(), calls=%async_computation.7 | async-start | bytes 4423680 | tf_op jit(solution)/shard_map/all_gather | solution.py:80
  81.6 2.9 %copy-start.3 = (f32[1280]{0:T(1024)S(1)}, f32[1280]{0:T(1024)}, u32[]{:S(2)}) copy-start(f32[1280]{0:T(1024)} %param.12) | copy-start | bytes 15364
  81.6 2.9 %copy-start.4 = (f32[1280]{0:T(1024)S(1)}, f32[1280]{0:T(1024)}, u32[]{:S(2)}) copy-start(f32[1280]{0:T(1024)} %param.11) | copy-start | bytes 15364
  101.8 129.1 %reduce-scatter.2.cloned.1.call-start = ((), (), s32[]{:S(2)}) async-start(), calls=%async_computation.6 | async-start | bytes 4423680 | tf_op jit(solution)/shard_map/reduce_scatter | solution.py:97
  150.7 3.1 %copy-start.1 = (bf16[2,1280,640]{2,1,0:T(8,128)(2,1)S(1)}, bf16[2,1280,640]{2,1,0:T(8,128)(2,1)}, u32[]{:S(2)}) copy-start(bf16[2,1280,640]{2,1,0:T(8,128)(2,1)} %param.14) | copy-start | bytes 9830404
  156.4 2.6 %copy-start.2 = (bf16[2,640,1280]{2,1,0:T(8,128)(2,1)S(1)}, bf16[2,640,1280]{2,1,0:T(8,128)(2,1)}, u32[]{:S(2)}) copy-start(bf16[2,640,1280]{2,1,0:T(8,128)(2,1)} %param.15) | copy-start | bytes 9830404
Sparse Core Ops, SparseCore 0:
  9.1 71.8 all-gather.3
  101.9 48.6 all-gather.5
  179.5 51.4 reduce-scatter.1

commit v3 on v2

--- a/solution.py
+++ b/solution.py
@@ -89,6 +89,7 @@
             ),
             approximate=False,
         ).astype(jnp.bfloat16)
+        hidden = lax.optimization_barrier(hidden)
         piece = jnp.einsum(
             "secf,fd->secd", hidden, expert_down[local], preferred_element_type=jnp.float32
         )

time: 257 us -> 255 us (level)
    dot_general x2, matrix products: 16.1 us -> 4.4 us  [per_device(): jnp.einsum('secf,fd->secd', hidden, expert_down[local], preferred_element...]
    dot_general x2, matrix products: 5.23 us -> 15 us  [per_device(): jnp.einsum('secd,df->secf', gathered[:, :, local], expert_up[local], pref...]
where the time goes in v3:
time: 255 us
  waiting for transfers between devices  153 us (60%)
  blocking collectives  32.8 us (13%)
  matrix products  26.8 us (11%)
  between operations  13.3 us (5%)
  local copies, waits for them, and re-layouts  12.8 us (5%)
  starting transfers between devices  12.2 us (5%)
  other arithmetic  3.41 us (1%)
    reduce_scatter x1, waiting for transfers between devices, per_device(): summed = lax.psum_scatter(pieces, 'seq', scatter_dimension=0, tiled=True)[0]  51.6 us
    all_gather x1, waiting for transfers between devices, per_device(): gathered = lax.all_gather(arrived, 'seq', axis=0, tiled=False)  48.6 us
    all_to_all x1, waiting for transfers between devices, per_device(): lax.all_to_all(token_minor, 'seq', split_axis=1, concat_axis=1, tiled=True)  36.7 us
    all_to_all x1, blocking collectives, per_device(): lax.all_to_all(summed, 'exp', split_axis=0, concat_axis=0, tiled=True)  16.5 us
    all_to_all x1, blocking collectives, per_device(): lax.all_to_all(dispatch, 'exp', split_axis=0, concat_axis=0, tiled=True)  16.3 us
    all_to_all x1, waiting for transfers between devices, per_device(): lax.all_to_all(attended, 'seq', split_axis=0, concat_axis=2, tiled=True)  15.7 us
    dot_general x2, matrix products, per_device(): jnp.einsum('secd,df->secf', gathered[:, :, local], expert_up[local], pref...  15 us
    all_to_all x1, starting transfers between devices, per_device(): lax.all_to_all(token_minor, 'seq', split_axis=1, concat_axis=1, tiled=True)  8.47 us
  transfers between devices with their start and end apart: 5, of which 4 were waited for; matrix products, arithmetic and copies ran while one was open for 4% of the time, Pallas kernels for 0%

profile of v3, /device:TPU:8, one launch (start us, length us, event | category | flops | bytes accessed | tf_op | source)
XLA Modules:
  0.0 254.7 jit_solution(1883152249794719823)
XLA Ops:
  6.5 0.0 all-gather.4.cloned.1.call-start
  6.5 0.7 all-gather.4.cloned.1.call-update
  7.3 1.6 copy.19
  8.9 1.0 copy.20
  9.9 8.5 %all-to-all-start = ((bf16[3,8,160,128]{3,2,0,1:T(8,128)(2,1)}), bf16[3,8,160,128]{3,2,0,1:T(8,128)(2,1)S(1)}, u32[]{:S(2)}, u32[]{:S(2)}) async-start(bf16[3,8,160,128]{3,2,0,1:T(8,128)(2,1)} %copy.20), calls=%async_computation | async-start | bytes 1966080 | tf_op jit(solution)/shard_map/all_to_all | solution.py:51
  18.4 36.7 %all-to-all-done = bf16[3,8,160,128]{3,2,0,1:T(8,128)(2,1)S(1)} async-done(((bf16[3,8,160,128]{3,2,0,1:T(8,128)(2,1)}), bf16[3,8,160,128]{3,2,0,1:T(8,128)(2,1)S(1)}, u32[]{:S(2)}, u32[]{:S(2)}) %all-to-all-start) | async-done | bytes 983072 | tf_op jit(solution)/shard_map/all_to_all | solution.py:51
  55.1 0.1 fusion.53
  55.2 1.3 multiply_reduce_fusion
  56.5 1.4 fusion
  57.8 0.0 copy-start
  57.9 2.0 fusion.40
  59.8 0.7 copy.28
  60.6 3.4 %all-to-all-start.1 = ((bf16[8,128,1,160]{1,3,2,0:T(8,128)(2,1)}), bf16[8,128,1,160]{1,3,2,0:T(8,128)(2,1)S(1)}, u32[]{:S(2)}, u32[]{:S(2)}) async-start(bf16[8,128,1,160]{1,3,2,0:T(8,128)(2,1)} %bitcast.13), calls=%async_computation.1 | async-start | bytes 655360 | tf_op jit(solution)/shard_map/all_to_all | solution.py:54
  64.0 0.0 all-gather.6.cloned.1.call-start
  64.1 0.7 dynamic-slice_bitcast_fusion
  64.8 0.1 fusion.51
  64.8 0.2 reduce_window_sum.11
  65.0 0.2 select_reduce_fusion
  65.2 0.7 multiply_add_fusion
  65.9 15.7 %all-to-all-done.1 = bf16[8,128,1,160]{1,3,2,0:T(8,128)(2,1)S(1)} async-done(((bf16[8,128,1,160]{1,3,2,0:T(8,128)(2,1)}), bf16[8,128,1,160]{1,3,2,0:T(8,128)(2,1)S(1)}, u32[]{:S(2)}, u32[]{:S(2)}) %all-to-all-start.1) | async-done | bytes 327712 | tf_op jit(solution)/shard_map/all_to_all | solution.py:54
  81.6 0.0 copy-done
  81.6 2.7 %fusion.54 = (f32[128]{0:T(128)S(1)}, f32[128,1280]{1,0:T(8,128)S(1)}) fusion(bf16[128,1280]{0,1:T(8,128)(2,1)S(1)} %bitcast.100, bf16[1280,1280]{1,0:T(8,128)(2,1)} %all-gather.4.cloned.1.call-done, bf16[1,128,1280]{2,1,0:T(8,128)(2,1)S(1)} %copy-done), kind=kOutput, calls=%fused_computation.88 | convolution fusion | flops 420249472 | bytes 4588032 | tf_op jit(solution)/shard_map/dot_general | solution.py:57
  84.3 0.2 multiply_reduce_fusion.1
  84.5 0.0 copy-done.3
  84.5 0.0 copy-done.4
  84.6 0.4 convolution_convert_fusion.2
  85.0 0.1 reshape.55
  85.1 0.4 copy.29
  85.5 16.3 %all_to_all.30 = bf16[8,2,12,1280]{3,1,2,0:T(2,128)(2,1)} all-to-all(bf16[8,2,12,1280]{3,1,2,0:T(2,128)(2,1)S(1)} %copy.29), channel_id=1, replica_groups=mesh['seq'=8,'exp'=8,'img'=4] {'exp'}, dimensions={0} | all-to-all | bytes 983040 | tf_op jit(solution)/shard_map/all_to_all | solution.py:79
  101.8 0.0 all-gather.6.cloned.1.call-update
  101.8 0.2 reduce-scatter.2.cloned.1.call-start
  102.0 48.6 %all-gather.6.cloned.1.call-done = bf16[64,2,12,1280]{3,1,2,0:T(2,128)(2,1)} async-done(((bf16[8,2,12,1280]{3,1,2,0:T(2,128)(2,1)}), bf16[64,2,12,1280]{3,1,2,0:T(2,128)(2,1)}) %all-gather.6.cloned.1.call-update) | async-done | bytes 3932176 | tf_op jit(solution)/shard_map/all_gather | solution.py:80
  150.7 3.0 %copy.30 = bf16[64,2,12,1280]{3,2,0,1:T(8,128)(2,1)S(1)} copy(bf16[64,2,12,1280]{3,1,2,0:T(2,128)(2,1)} %all-gather.6.cloned.1.call-done) | data formatting | bytes 7864320 | tf_op jit(solution)/shard_map/all_gather | solution.py:80
  153.7 0.1 copy-done.1
  153.8 7.4 %fusion.6 = bf16[8,8,12,640]{3,2,1,0:T(8,128)(2,1)S(1)} fusion(bf16[2,1280,640]{2,1,0:T(8,128)(2,1)S(1)} %copy-done.1, bf16[8,8,2,12,1280]{4,3,1,0,2:T(8,128)(2,1)S(1)} %bitcast.97), kind=kOutput, calls=%fused_computation.14 | convolution fusion | flops 1290240000 | bytes 5242880 | tf_op jit(solution)/shard_map/secd,df->secf/dot_general | solution.py:84
  161.2 0.0 copy-start.2
  161.2 7.6 %fusion.9 = bf16[8,8,12,640]{3,2,1,0:T(8,128)(2,1)S(1)} fusion(bf16[2,1280,640]{2,1,0:T(8,128)(2,1)S(1)} %copy-done.1, bf16[8,8,2,12,1280]{4,3,1,0,2:T(8,128)(2,1)S(1)} %bitcast.98), kind=kOutput, calls=%fused_computation.17 | convolution fusion | flops 1290240000 | bytes 5242880 | tf_op jit(solution)/shard_map/secd,df->secf/dot_general | solution.py:84
  168.8 2.2 fusion.2
  171.0 2.2 fusion.3
  173.2 0.7 pad_maximum_fusion
  174.0 3.4 %copy.31 = bf16[8,8,2,12,1280]{4,1,3,2,0:T(8,128)(2,1)} copy(bf16[8,8,2,12,1280]{4,3,1,0,2:T(8,128)(2,1)S(1)} %pad_maximum_fusion) | data formatting | bytes 7864320 | tf_op jit(solution)/shard_map/stack | solution.py:97
  177.4 0.0 reduce-scatter.2.cloned.1.call-update
  177.4 51.6 %reduce-scatter.2.cloned.1.call-done = bf16[1,8,2,12,1280]{4,1,3,2,0:T(8,128)(2,1)} async-done(((bf16[8,8,2,12,1280]{4,1,3,2,0:T(8,128)(2,1)}), bf16[1,8,2,12,1280]{4,1,3,2,0:T(8,128)(2,1)}) %reduce-scatter.2.cloned.1.call-update) | async-done | bytes 491536 | tf_op jit(solution)/shard_map/reduce_scatter | solution.py:98
  229.0 1.5 copy.32
  230.5 16.5 %all_to_all.31 = bf16[8,2,12,1280]{3,1,2,0:T(2,128)(2,1)S(1)} all-to-all(bf16[8,2,12,1280]{3,1,2,0:T(2,128)(2,1)S(1)} %copy.32), channel_id=1, replica_groups=mesh['seq'=8,'exp'=8,'img'=4] {'exp'}, dimensions={0} | all-to-all | bytes 983040 | tf_op jit(solution)/shard_map/all_to_all | solution.py:99
  247.0 0.1 copy.33
  247.1 0.1 reshape.56
  247.2 1.0 fusion.29
  (7 shorter events, 0.0 us)
Async XLA Ops:
  6.5 75.1 %all-gather.4.cloned.1.call-start = ((), (), s32[]{:S(2)}) async-start(), calls=%async_computation.5 | async-start | bytes 3686400 | tf_op jit(solution)/shard_map/all_gather | solution.py:59
  9.9 45.2 %all-to-all-start = ((bf16[3,8,160,128]{3,2,0,1:T(8,128)(2,1)}), bf16[3,8,160,128]{3,2,0,1:T(8,128)(2,1)S(1)}, u32[]{:S(2)}, u32[]{:S(2)}) async-start(bf16[3,8,160,128]{3,2,0,1:T(8,128)(2,1)} %copy.20), calls=%async_computation | async-start | bytes 1966080 | tf_op jit(solution)/shard_map/all_to_all | solution.py:51
  57.8 23.8 %copy-start = (bf16[1,128,1280]{2,1,0:T(8,128)(2,1)S(1)}, bf16[1,128,1280]{2,1,0:T(8,128)(2,1)}, u32[]{:S(2)}) copy-start(bf16[1,128,1280]{2,1,0:T(8,128)(2,1)} %param.9) | copy-start | bytes 983044
  60.6 21.0 %all-to-all-start.1 = ((bf16[8,128,1,160]{1,3,2,0:T(8,128)(2,1)}), bf16[8,128,1,160]{1,3,2,0:T(8,128)(2,1)S(1)}, u32[]{:S(2)}, u32[]{:S(2)}) async-start(bf16[8,128,1,160]{1,3,2,0:T(8,128)(2,1)} %bitcast.13), calls=%async_computation.1 | async-start | bytes 655360 | tf_op jit(solution)/shard_map/all_to_all | solution.py:54
  64.0 86.6 %all-gather.6.cloned.1.call-start = ((), (), s32[]{:S(2)}) async-start(), calls=%async_computation.7 | async-start | bytes 4423680 | tf_op jit(solution)/shard_map/all_gather | solution.py:80
  81.6 2.9 %copy-start.3 = (f32[1280]{0:T(1024)S(1)}, f32[1280]{0:T(1024)}, u32[]{:S(2)}) copy-start(f32[1280]{0:T(1024)} %param.12) | copy-start | bytes 15364
  81.6 2.9 %copy-start.4 = (f32[1280]{0:T(1024)S(1)}, f32[1280]{0:T(1024)}, u32[]{:S(2)}) copy-start(f32[1280]{0:T(1024)} %param.11) | copy-start | bytes 15364
  101.8 127.2 %reduce-scatter.2.cloned.1.call-start = ((), (), s32[]{:S(2)}) async-start(), calls=%async_computation.6 | async-start | bytes 4423680 | tf_op jit(solution)/shard_map/reduce_scatter | solution.py:98
  150.7 3.1 %copy-start.1 = (bf16[2,1280,640]{2,1,0:T(8,128)(2,1)S(1)}, bf16[2,1280,640]{2,1,0:T(8,128)(2,1)}, u32[]{:S(2)}) copy-start(bf16[2,1280,640]{2,1,0:T(8,128)(2,1)} %param.14) | copy-start | bytes 9830404
  161.2 7.7 %copy-start.2 = (bf16[2,640,1280]{2,1,0:T(8,128)(2,1)S(1)}, bf16[2,640,1280]{2,1,0:T(8,128)(2,1)}, u32[]{:S(2)}) copy-start(bf16[2,640,1280]{2,1,0:T(8,128)(2,1)} %param.15) | copy-start | bytes 9830404
Sparse Core Ops, SparseCore 0:
  9.1 71.8 all-gather.3
  101.9 48.6 all-gather.5
  177.5 51.4 reduce-scatter.1

commit v4 on v3

--- a/solution.py
+++ b/solution.py
@@ -71,11 +71,10 @@
     dest = ids_own * cap_dev + order_in_block
     select = (dest[:, None] == jnp.arange(experts * cap_dev, dtype=jnp.int32)[None, :]).astype(
         jnp.bfloat16
-    )
+    ).reshape(tok_rows, exp_count, local_experts, cap_dev)
     dispatch = jnp.einsum(
-        "tk,td->kd", select, normed, preferred_element_type=jnp.float32
+        "tgjc,td->gjcd", select, normed, preferred_element_type=jnp.float32
     ).astype(jnp.bfloat16)
-    dispatch = dispatch.reshape(exp_count, local_experts, cap_dev, model_width)
     arrived = lax.all_to_all(dispatch, "exp", split_axis=0, concat_axis=0, tiled=True)
     gathered = lax.all_gather(arrived, "seq", axis=0, tiled=False)
     pieces = []
@@ -96,10 +95,10 @@
         pieces.append(piece.astype(jnp.bfloat16))
     pieces = jnp.stack(pieces, axis=2)
     summed = lax.psum_scatter(pieces, "seq", scatter_dimension=0, tiled=True)[0]
-    returned = lax.all_to_all(summed, "exp", split_axis=0, concat_axis=0, tiled=True).reshape(
-        experts * cap_dev, model_width
+    returned = lax.all_to_all(summed, "exp", split_axis=0, concat_axis=0, tiled=True)
+    expert_out = jnp.einsum(
+        "tgjc,gjcd->td", select, returned, preferred_element_type=jnp.float32
     )
-    expert_out = jnp.einsum("tk,kd->td", select, returned, preferred_element_type=jnp.float32)
     return (stream_own + expert_out).astype(jnp.bfloat16)[None]
 
 

time: 255 us -> 255 us (level)
  no operation moved by 1% of the time
where the time goes in v4:
time: 255 us
  waiting for transfers between devices  153 us (60%)
  blocking collectives  32.8 us (13%)
  matrix products  26.9 us (11%)
  between operations  13.3 us (5%)
  local copies, waits for them, and re-layouts  12.5 us (5%)
  starting transfers between devices  12.2 us (5%)
  other arithmetic  3.42 us (1%)
    reduce_scatter x1, waiting for transfers between devices, per_device(): summed = lax.psum_scatter(pieces, 'seq', scatter_dimension=0, tiled=True)[0]  51.6 us
    all_gather x1, waiting for transfers between devices, per_device(): gathered = lax.all_gather(arrived, 'seq', axis=0, tiled=False)  48.6 us
    all_to_all x1, waiting for transfers between devices, per_device(): lax.all_to_all(token_minor, 'seq', split_axis=1, concat_axis=1, tiled=True)  36.1 us
    all_to_all x1, blocking collectives, per_device(): lax.all_to_all(summed, 'exp', split_axis=0, concat_axis=0, tiled=True)  16.5 us
    all_to_all x1, waiting for transfers between devices, per_device(): lax.all_to_all(attended, 'seq', split_axis=0, concat_axis=2, tiled=True)  16.4 us
    all_to_all x1, blocking collectives, per_device(): lax.all_to_all(dispatch, 'exp', split_axis=0, concat_axis=0, tiled=True)  16.3 us
    dot_general x2, matrix products, per_device(): jnp.einsum('secd,df->secf', gathered[:, :, local], expert_up[local], pref...  15 us
    all_to_all x1, starting transfers between devices, per_device(): lax.all_to_all(token_minor, 'seq', split_axis=1, concat_axis=1, tiled=True)  8.47 us
  transfers between devices with their start and end apart: 5, of which 4 were waited for; matrix products, arithmetic and copies ran while one was open for 4% of the time, Pallas kernels for 0%

profile of v4, /device:TPU:8, one launch (start us, length us, event | category | flops | bytes accessed | tf_op | source)
XLA Modules:
  0.0 254.5 jit_solution(2176407205508284197)
XLA Ops:
  6.5 0.0 all-gather.4.cloned.1.call-start
  6.5 0.7 all-gather.4.cloned.1.call-update
  7.3 1.6 copy.22
  8.9 1.0 copy.23
  9.9 8.5 %all-to-all-start = ((bf16[3,8,160,128]{3,2,0,1:T(8,128)(2,1)}), bf16[3,8,160,128]{3,2,0,1:T(8,128)(2,1)S(1)}, u32[]{:S(2)}, u32[]{:S(2)}) async-start(bf16[3,8,160,128]{3,2,0,1:T(8,128)(2,1)} %copy.23), calls=%async_computation | async-start | bytes 1966080 | tf_op jit(solution)/shard_map/all_to_all | solution.py:51
  18.4 0.7 dynamic-slice_bitcast_fusion
  19.0 36.1 %all-to-all-done = bf16[3,8,160,128]{3,2,0,1:T(8,128)(2,1)S(1)} async-done(((bf16[3,8,160,128]{3,2,0,1:T(8,128)(2,1)}), bf16[3,8,160,128]{3,2,0,1:T(8,128)(2,1)S(1)}, u32[]{:S(2)}, u32[]{:S(2)}) %all-to-all-start) | async-done | bytes 983072 | tf_op jit(solution)/shard_map/all_to_all | solution.py:51
  55.1 0.1 fusion.63
  55.2 1.3 multiply_reduce_fusion
  56.5 1.4 fusion
  57.8 0.0 copy-start
  57.9 2.0 fusion.41
  59.8 0.7 copy.31
  60.6 3.4 %all-to-all-start.1 = ((bf16[8,128,1,160]{1,3,2,0:T(8,128)(2,1)}), bf16[8,128,1,160]{1,3,2,0:T(8,128)(2,1)S(1)}, u32[]{:S(2)}, u32[]{:S(2)}) async-start(bf16[8,128,1,160]{1,3,2,0:T(8,128)(2,1)} %bitcast.13), calls=%async_computation.1 | async-start | bytes 655360 | tf_op jit(solution)/shard_map/all_to_all | solution.py:54
  64.0 0.0 all-gather.6.cloned.1.call-start
  64.1 0.1 fusion.61
  64.2 0.2 reduce_window_sum.11
  64.4 0.2 select_reduce_fusion
  64.5 0.7 multiply_add_fusion.1
  65.2 16.4 %all-to-all-done.1 = bf16[8,128,1,160]{1,3,2,0:T(8,128)(2,1)S(1)} async-done(((bf16[8,128,1,160]{1,3,2,0:T(8,128)(2,1)}), bf16[8,128,1,160]{1,3,2,0:T(8,128)(2,1)S(1)}, u32[]{:S(2)}, u32[]{:S(2)}) %all-to-all-start.1) | async-done | bytes 327712 | tf_op jit(solution)/shard_map/all_to_all | solution.py:54
  81.6 0.0 all-gather.4.cloned.1.call-done
  81.6 0.0 copy-done
  81.6 0.0 copy-start.3
  81.6 2.7 %fusion.64 = (f32[128]{0:T(128)S(1)}, f32[128,1280]{1,0:T(8,128)S(1)}) fusion(bf16[128,1280]{0,1:T(8,128)(2,1)S(1)} %bitcast.114, bf16[1280,1280]{1,0:T(8,128)(2,1)} %all-gather.4.cloned.1.call-done, bf16[1,128,1280]{2,1,0:T(8,128)(2,1)S(1)} %copy-done), kind=kOutput, calls=%fused_computation.98 | convolution fusion | flops 420249472 | bytes 4588032 | tf_op jit(solution)/shard_map/dot_general | solution.py:57
  84.3 0.2 multiply_reduce_fusion.1
  84.5 0.0 copy-done.3
  84.5 0.0 copy-done.4
  84.6 0.4 convolution_convert_fusion.2
  85.0 0.4 copy.32
  85.4 16.3 %all_to_all.30 = bf16[8,2,12,1280]{3,1,2,0:T(2,128)(2,1)} all-to-all(bf16[8,2,12,1280]{3,1,2,0:T(2,128)(2,1)S(1)} %copy.32), channel_id=1, replica_groups=mesh['seq'=8,'exp'=8,'img'=4] {'exp'}, dimensions={0} | all-to-all | bytes 983040 | tf_op jit(solution)/shard_map/all_to_all | solution.py:78
  101.7 0.0 all-gather.6.cloned.1.call-update
  101.7 0.2 reduce-scatter.2.cloned.1.call-start
  102.0 48.6 %all-gather.6.cloned.1.call-done = bf16[64,2,12,1280]{3,1,2,0:T(2,128)(2,1)} async-done(((bf16[8,2,12,1280]{3,1,2,0:T(2,128)(2,1)}), bf16[64,2,12,1280]{3,1,2,0:T(2,128)(2,1)}) %all-gather.6.cloned.1.call-update) | async-done | bytes 3932176 | tf_op jit(solution)/shard_map/all_gather | solution.py:79
  150.6 3.0 %copy.33 = bf16[64,2,12,1280]{3,2,0,1:T(8,128)(2,1)S(1)} copy(bf16[64,2,12,1280]{3,1,2,0:T(2,128)(2,1)} %all-gather.6.cloned.1.call-done) | data formatting | bytes 7864320 | tf_op jit(solution)/shard_map/all_gather | solution.py:79
  153.6 0.1 copy-done.1
  153.7 7.4 %fusion.6 = bf16[8,8,12,640]{3,2,1,0:T(8,128)(2,1)S(1)} fusion(bf16[2,1280,640]{2,1,0:T(8,128)(2,1)S(1)} %copy-done.1, bf16[8,8,2,12,1280]{4,3,1,0,2:T(8,128)(2,1)S(1)} %bitcast.111), kind=kOutput, calls=%fused_computation.14 | convolution fusion | flops 1290240000 | bytes 5242880 | tf_op jit(solution)/shard_map/secd,df->secf/dot_general | solution.py:83
  161.1 0.0 copy-start.2
  161.1 7.6 %fusion.9 = bf16[8,8,12,640]{3,2,1,0:T(8,128)(2,1)S(1)} fusion(bf16[2,1280,640]{2,1,0:T(8,128)(2,1)S(1)} %copy-done.1, bf16[8,8,2,12,1280]{4,3,1,0,2:T(8,128)(2,1)S(1)} %bitcast.112), kind=kOutput, calls=%fused_computation.17 | convolution fusion | flops 1290240000 | bytes 5242880 | tf_op jit(solution)/shard_map/secd,df->secf/dot_general | solution.py:83
  168.7 0.0 copy-done.2
  168.7 2.2 fusion.2
  170.9 2.2 fusion.3
  173.1 0.7 pad_maximum_fusion
  173.9 3.4 %copy.34 = bf16[8,8,2,12,1280]{4,1,3,2,0:T(8,128)(2,1)} copy(bf16[8,8,2,12,1280]{4,3,1,0,2:T(8,128)(2,1)S(1)} %pad_maximum_fusion) | data formatting | bytes 7864320 | tf_op jit(solution)/shard_map/stack | solution.py:96
  177.3 0.0 reduce-scatter.2.cloned.1.call-update
  177.3 51.6 %reduce-scatter.2.cloned.1.call-done = bf16[1,8,2,12,1280]{4,1,3,2,0:T(8,128)(2,1)} async-done(((bf16[8,8,2,12,1280]{4,1,3,2,0:T(8,128)(2,1)}), bf16[1,8,2,12,1280]{4,1,3,2,0:T(8,128)(2,1)}) %reduce-scatter.2.cloned.1.call-update) | async-done | bytes 491536 | tf_op jit(solution)/shard_map/reduce_scatter | solution.py:97
  228.9 1.5 copy.35
  230.4 16.5 %all_to_all.31 = bf16[8,2,12,1280]{3,1,2,0:T(2,128)(2,1)S(1)} all-to-all(bf16[8,2,12,1280]{3,1,2,0:T(2,128)(2,1)S(1)} %copy.35), channel_id=1, replica_groups=mesh['seq'=8,'exp'=8,'img'=4] {'exp'}, dimensions={0} | all-to-all | bytes 983040 | tf_op jit(solution)/shard_map/all_to_all | solution.py:98
  246.9 1.1 fusion.30
  (5 shorter events, 0.0 us)
Async XLA Ops:
  6.5 75.1 %all-gather.4.cloned.1.call-start = ((), (), s32[]{:S(2)}) async-start(), calls=%async_computation.5 | async-start | bytes 3686400 | tf_op jit(solution)/shard_map/all_gather | solution.py:59
  9.9 45.2 %all-to-all-start = ((bf16[3,8,160,128]{3,2,0,1:T(8,128)(2,1)}), bf16[3,8,160,128]{3,2,0,1:T(8,128)(2,1)S(1)}, u32[]{:S(2)}, u32[]{:S(2)}) async-start(bf16[3,8,160,128]{3,2,0,1:T(8,128)(2,1)} %copy.23), calls=%async_computation | async-start | bytes 1966080 | tf_op jit(solution)/shard_map/all_to_all | solution.py:51
  57.8 23.8 %copy-start = (bf16[1,128,1280]{2,1,0:T(8,128)(2,1)S(1)}, bf16[1,128,1280]{2,1,0:T(8,128)(2,1)}, u32[]{:S(2)}) copy-start(bf16[1,128,1280]{2,1,0:T(8,128)(2,1)} %param.9) | copy-start | bytes 983044
  60.6 21.0 %all-to-all-start.1 = ((bf16[8,128,1,160]{1,3,2,0:T(8,128)(2,1)}), bf16[8,128,1,160]{1,3,2,0:T(8,128)(2,1)S(1)}, u32[]{:S(2)}, u32[]{:S(2)}) async-start(bf16[8,128,1,160]{1,3,2,0:T(8,128)(2,1)} %bitcast.13), calls=%async_computation.1 | async-start | bytes 655360 | tf_op jit(solution)/shard_map/all_to_all | solution.py:54
  64.0 86.5 %all-gather.6.cloned.1.call-start = ((), (), s32[]{:S(2)}) async-start(), calls=%async_computation.7 | async-start | bytes 4423680 | tf_op jit(solution)/shard_map/all_gather | solution.py:79
  81.6 2.9 %copy-start.3 = (f32[1280]{0:T(1024)S(1)}, f32[1280]{0:T(1024)}, u32[]{:S(2)}) copy-start(f32[1280]{0:T(1024)} %param.12) | copy-start | bytes 15364
  81.6 2.9 %copy-start.4 = (f32[1280]{0:T(1024)S(1)}, f32[1280]{0:T(1024)}, u32[]{:S(2)}) copy-start(f32[1280]{0:T(1024)} %param.11) | copy-start | bytes 15364
  101.7 127.2 %reduce-scatter.2.cloned.1.call-start = ((), (), s32[]{:S(2)}) async-start(), calls=%async_computation.6 | async-start | bytes 4423680 | tf_op jit(solution)/shard_map/reduce_scatter | solution.py:97
  150.6 3.1 %copy-start.1 = (bf16[2,1280,640]{2,1,0:T(8,128)(2,1)S(1)}, bf16[2,1280,640]{2,1,0:T(8,128)(2,1)}, u32[]{:S(2)}) copy-start(bf16[2,1280,640]{2,1,0:T(8,128)(2,1)} %param.14) | copy-start | bytes 9830404
  161.1 7.6 %copy-start.2 = (bf16[2,640,1280]{2,1,0:T(8,128)(2,1)S(1)}, bf16[2,640,1280]{2,1,0:T(8,128)(2,1)}, u32[]{:S(2)}) copy-start(bf16[2,640,1280]{2,1,0:T(8,128)(2,1)} %param.15) | copy-start | bytes 9830404
Sparse Core Ops, SparseCore 0:
  9.1 71.8 all-gather.3
  101.8 48.6 all-gather.5
  177.4 51.4 reduce-scatter.1

commit v5 on v4

--- a/solution.py
+++ b/solution.py
@@ -79,15 +79,13 @@
     gathered = lax.all_gather(arrived, "seq", axis=0, tiled=False)
     pieces = []
     for local in range(local_experts):
-        hidden = jax.nn.gelu(
-            jnp.einsum(
-                "secd,df->secf",
-                gathered[:, :, local],
-                expert_up[local],
-                preferred_element_type=jnp.float32,
-            ),
-            approximate=False,
-        ).astype(jnp.bfloat16)
+        lifted = jnp.einsum(
+            "secd,df->secf",
+            gathered[:, :, local],
+            expert_up[local],
+            preferred_element_type=jnp.float32,
+        )
+        hidden = (0.5 * lifted * (1.0 + lax.erf(lifted * (0.5**0.5)))).astype(jnp.bfloat16)
         hidden = lax.optimization_barrier(hidden)
         piece = jnp.einsum(
             "secf,fd->secd", hidden, expert_down[local], preferred_element_type=jnp.float32

time: 255 us -> 245 us (0.961)
  matrix products: 26.9 us -> 16.8 us
    dot_general x2, matrix products: 15 us -> 4.87 us  [per_device(): jnp.einsum('secd,df->secf', gathered[:, :, local], expert_up[local], pref...]
where the time goes in v5:
time: 245 us; the launch traced here: 244 us
  waiting for transfers between devices  153 us (62%)
  blocking collectives  32.8 us (13%)
  matrix products  16.8 us (7%)
  between operations  13.3 us (5%)
  local copies, waits for them, and re-layouts  12.5 us (5%)
  starting transfers between devices  12.2 us (5%)
  other arithmetic  3.42 us (1%)
    reduce_scatter x1, waiting for transfers between devices, per_device(): summed = lax.psum_scatter(pieces, 'seq', scatter_dimension=0, tiled=True)[0]  51.6 us
    all_gather x1, waiting for transfers between devices, per_device(): gathered = lax.all_gather(arrived, 'seq', axis=0, tiled=False)  48.6 us
    all_to_all x1, waiting for transfers between devices, per_device(): lax.all_to_all(token_minor, 'seq', split_axis=1, concat_axis=1, tiled=True)  36.1 us
    all_to_all x1, blocking collectives, per_device(): lax.all_to_all(summed, 'exp', split_axis=0, concat_axis=0, tiled=True)  16.5 us
    all_to_all x1, waiting for transfers between devices, per_device(): lax.all_to_all(attended, 'seq', split_axis=0, concat_axis=2, tiled=True)  16.4 us
    all_to_all x1, blocking collectives, per_device(): lax.all_to_all(dispatch, 'exp', split_axis=0, concat_axis=0, tiled=True)  16.3 us
    all_to_all x1, starting transfers between devices, per_device(): lax.all_to_all(token_minor, 'seq', split_axis=1, concat_axis=1, tiled=True)  8.47 us
  transfers between devices with their start and end apart: 5, of which 4 were waited for; matrix products, arithmetic and copies ran while one was open for 4% of the time, Pallas kernels for 0%

profile of v5, /device:TPU:8, one launch (start us, length us, event | category | flops | bytes accessed | tf_op | source)
XLA Modules:
  0.0 244.4 jit_solution(7343234804195419089)
XLA Ops:
  6.5 0.0 all-gather.4.cloned.1.call-start
  6.5 0.7 all-gather.4.cloned.1.call-update
  7.3 1.6 copy.22
  8.9 1.0 copy.23
  9.9 8.5 %all-to-all-start = ((bf16[3,8,160,128]{3,2,0,1:T(8,128)(2,1)}), bf16[3,8,160,128]{3,2,0,1:T(8,128)(2,1)S(1)}, u32[]{:S(2)}, u32[]{:S(2)}) async-start(bf16[3,8,160,128]{3,2,0,1:T(8,128)(2,1)} %copy.23), calls=%async_computation | async-start | bytes 1966080 | tf_op jit(solution)/shard_map/all_to_all | solution.py:51
  18.4 0.7 dynamic-slice_bitcast_fusion
  19.0 36.1 %all-to-all-done = bf16[3,8,160,128]{3,2,0,1:T(8,128)(2,1)S(1)} async-done(((bf16[3,8,160,128]{3,2,0,1:T(8,128)(2,1)}), bf16[3,8,160,128]{3,2,0,1:T(8,128)(2,1)S(1)}, u32[]{:S(2)}, u32[]{:S(2)}) %all-to-all-start) | async-done | bytes 983072 | tf_op jit(solution)/shard_map/all_to_all | solution.py:51
  55.1 0.1 fusion.43
  55.2 1.3 multiply_reduce_fusion
  56.5 1.4 fusion
  57.8 0.0 copy-start
  57.9 2.0 fusion.25
  59.8 0.0 copy-start.3
  59.9 0.0 copy-start.4
  59.9 0.7 copy.31
  60.6 3.4 %all-to-all-start.1 = ((bf16[8,128,1,160]{1,3,2,0:T(8,128)(2,1)}), bf16[8,128,1,160]{1,3,2,0:T(8,128)(2,1)S(1)}, u32[]{:S(2)}, u32[]{:S(2)}) async-start(bf16[8,128,1,160]{1,3,2,0:T(8,128)(2,1)} %bitcast.13), calls=%async_computation.1 | async-start | bytes 655360 | tf_op jit(solution)/shard_map/all_to_all | solution.py:54
  64.1 0.0 all-gather.6.cloned.1.call-start
  64.1 0.1 fusion.41
  64.2 0.2 reduce_window_sum.11
  64.4 0.2 select_reduce_fusion
  64.6 0.7 multiply_add_fusion.1
  65.2 16.4 %all-to-all-done.1 = bf16[8,128,1,160]{1,3,2,0:T(8,128)(2,1)S(1)} async-done(((bf16[8,128,1,160]{1,3,2,0:T(8,128)(2,1)}), bf16[8,128,1,160]{1,3,2,0:T(8,128)(2,1)S(1)}, u32[]{:S(2)}, u32[]{:S(2)}) %all-to-all-start.1) | async-done | bytes 327712 | tf_op jit(solution)/shard_map/all_to_all | solution.py:54
  81.6 0.0 copy-done
  81.6 2.6 %fusion.44 = (f32[128]{0:T(128)S(1)}, f32[128,1280]{1,0:T(8,128)S(1)}) fusion(bf16[128,1280]{0,1:T(8,128)(2,1)S(1)} %bitcast.114, bf16[1280,1280]{1,0:T(8,128)(2,1)} %all-gather.4.cloned.1.call-done, bf16[1,128,1280]{2,1,0:T(8,128)(2,1)S(1)} %copy-done), kind=kOutput, calls=%fused_computation.62 | convolution fusion | flops 420249472 | bytes 4588032 | tf_op jit(solution)/shard_map/dot_general | solution.py:57
  84.3 0.2 multiply_reduce_fusion.1
  84.5 0.0 copy-done.3
  84.5 0.0 copy-done.4
  84.5 0.4 convolution_convert_fusion.2
  85.0 0.4 copy.32
  85.4 16.3 %all_to_all.30 = bf16[8,2,12,1280]{3,1,2,0:T(2,128)(2,1)} all-to-all(bf16[8,2,12,1280]{3,1,2,0:T(2,128)(2,1)S(1)} %copy.32), channel_id=1, replica_groups=mesh['seq'=8,'exp'=8,'img'=4] {'exp'}, dimensions={0} | all-to-all | bytes 983040 | tf_op jit(solution)/shard_map/all_to_all | solution.py:78
  101.7 0.0 all-gather.6.cloned.1.call-update
  101.7 0.2 reduce-scatter.2.cloned.1.call-start
  101.9 48.6 %all-gather.6.cloned.1.call-done = bf16[64,2,12,1280]{3,1,2,0:T(2,128)(2,1)} async-done(((bf16[8,2,12,1280]{3,1,2,0:T(2,128)(2,1)}), bf16[64,2,12,1280]{3,1,2,0:T(2,128)(2,1)}) %all-gather.6.cloned.1.call-update) | async-done | bytes 3932176 | tf_op jit(solution)/shard_map/all_gather | solution.py:79
  150.5 3.0 %copy.33 = bf16[64,2,12,1280]{3,2,0,1:T(8,128)(2,1)S(1)} copy(bf16[64,2,12,1280]{3,1,2,0:T(2,128)(2,1)} %all-gather.6.cloned.1.call-done) | data formatting | bytes 7864320 | tf_op jit(solution)/shard_map/all_gather | solution.py:79
  153.5 0.1 copy-done.1
  153.6 2.4 multiply_convert_fusion.1
  156.1 0.0 copy-start.2
  156.1 2.4 multiply_convert_fusion
  158.5 0.0 copy-done.2
  158.5 2.2 fusion.2
  160.8 2.2 fusion.3
  163.0 0.7 pad_maximum_fusion
  163.7 3.4 %copy.34 = bf16[8,8,2,12,1280]{4,1,3,2,0:T(8,128)(2,1)} copy(bf16[8,8,2,12,1280]{4,3,1,0,2:T(8,128)(2,1)S(1)} %pad_maximum_fusion) | data formatting | bytes 7864320 | tf_op jit(solution)/shard_map/stack | solution.py:94
  167.1 0.0 reduce-scatter.2.cloned.1.call-update
  167.1 51.6 %reduce-scatter.2.cloned.1.call-done = bf16[1,8,2,12,1280]{4,1,3,2,0:T(8,128)(2,1)} async-done(((bf16[8,8,2,12,1280]{4,1,3,2,0:T(8,128)(2,1)}), bf16[1,8,2,12,1280]{4,1,3,2,0:T(8,128)(2,1)}) %reduce-scatter.2.cloned.1.call-update) | async-done | bytes 491536 | tf_op jit(solution)/shard_map/reduce_scatter | solution.py:95
  218.7 1.5 copy.35
  220.2 16.5 %all_to_all.31 = bf16[8,2,12,1280]{3,1,2,0:T(2,128)(2,1)S(1)} all-to-all(bf16[8,2,12,1280]{3,1,2,0:T(2,128)(2,1)S(1)} %copy.35), channel_id=1, replica_groups=mesh['seq'=8,'exp'=8,'img'=4] {'exp'}, dimensions={0} | all-to-all | bytes 983040 | tf_op jit(solution)/shard_map/all_to_all | solution.py:96
  236.7 1.1 fusion.10
  (5 shorter events, 0.0 us)
Async XLA Ops:
  6.5 75.1 %all-gather.4.cloned.1.call-start = ((), (), s32[]{:S(2)}) async-start(), calls=%async_computation.5 | async-start | bytes 3686400 | tf_op jit(solution)/shard_map/all_gather | solution.py:59
  9.9 45.2 %all-to-all-start = ((bf16[3,8,160,128]{3,2,0,1:T(8,128)(2,1)}), bf16[3,8,160,128]{3,2,0,1:T(8,128)(2,1)S(1)}, u32[]{:S(2)}, u32[]{:S(2)}) async-start(bf16[3,8,160,128]{3,2,0,1:T(8,128)(2,1)} %copy.23), calls=%async_computation | async-start | bytes 1966080 | tf_op jit(solution)/shard_map/all_to_all | solution.py:51
  57.8 23.8 %copy-start = (bf16[1,128,1280]{2,1,0:T(8,128)(2,1)S(1)}, bf16[1,128,1280]{2,1,0:T(8,128)(2,1)}, u32[]{:S(2)}) copy-start(bf16[1,128,1280]{2,1,0:T(8,128)(2,1)} %param.9) | copy-start | bytes 983044
  59.8 24.7 %copy-start.3 = (f32[1280]{0:T(1024)S(1)}, f32[1280]{0:T(1024)}, u32[]{:S(2)}) copy-start(f32[1280]{0:T(1024)} %param.12) | copy-start | bytes 15364
  59.9 24.7 %copy-start.4 = (f32[1280]{0:T(1024)S(1)}, f32[1280]{0:T(1024)}, u32[]{:S(2)}) copy-start(f32[1280]{0:T(1024)} %param.11) | copy-start | bytes 15364
  60.6 21.0 %all-to-all-start.1 = ((bf16[8,128,1,160]{1,3,2,0:T(8,128)(2,1)}), bf16[8,128,1,160]{1,3,2,0:T(8,128)(2,1)S(1)}, u32[]{:S(2)}, u32[]{:S(2)}) async-start(bf16[8,128,1,160]{1,3,2,0:T(8,128)(2,1)} %bitcast.13), calls=%async_computation.1 | async-start | bytes 655360 | tf_op jit(solution)/shard_map/all_to_all | solution.py:54
  64.1 86.5 %all-gather.6.cloned.1.call-start = ((), (), s32[]{:S(2)}) async-start(), calls=%async_computation.7 | async-start | bytes 4423680 | tf_op jit(solution)/shard_map/all_gather | solution.py:79
  101.7 117.0 %reduce-scatter.2.cloned.1.call-start = ((), (), s32[]{:S(2)}) async-start(), calls=%async_computation.6 | async-start | bytes 4423680 | tf_op jit(solution)/shard_map/reduce_scatter | solution.py:95
  150.5 3.1 %copy-start.1 = (bf16[2,1280,640]{2,1,0:T(8,128)(2,1)S(1)}, bf16[2,1280,640]{2,1,0:T(8,128)(2,1)}, u32[]{:S(2)}) copy-start(bf16[2,1280,640]{2,1,0:T(8,128)(2,1)} %param.14) | copy-start | bytes 9830404
  156.1 2.5 %copy-start.2 = (bf16[2,640,1280]{2,1,0:T(8,128)(2,1)S(1)}, bf16[2,640,1280]{2,1,0:T(8,128)(2,1)}, u32[]{:S(2)}) copy-start(bf16[2,640,1280]{2,1,0:T(8,128)(2,1)} %param.15) | copy-start | bytes 9830404
Sparse Core Ops, SparseCore 0:
  9.1 71.8 all-gather.3
  101.8 48.6 all-gather.5
  167.2 51.4 reduce-scatter.1

commit v6 on v5

--- a/solution.py
+++ b/solution.py
@@ -54,10 +54,22 @@
     token_heads = lax.all_to_all(attended, "seq", split_axis=0, concat_axis=2, tiled=True).reshape(
         tok_rows, model_width
     )
-    projected_sum = jnp.dot(
-        token_heads,
-        lax.all_gather(attn_proj, "seq", axis=0, tiled=True),
-        preferred_element_type=jnp.float32,
+    img_count = lax.axis_size("img")
+    core = lax.axis_index("img") % 2
+    half_width = model_width // 2
+    proj_half = lax.all_gather(
+        lax.dynamic_slice_in_dim(attn_proj, core * half_width, half_width, axis=1),
+        "seq",
+        axis=0,
+        tiled=True,
+    )
+    proj_other = lax.ppermute(proj_half, "img", [(i, i ^ 1) for i in range(img_count)])
+    sum_half = jnp.dot(token_heads, proj_half, preferred_element_type=jnp.float32)
+    sum_other = jnp.dot(token_heads, proj_other, preferred_element_type=jnp.float32)
+    projected_sum = jnp.where(
+        core == 0,
+        jnp.concatenate([sum_half, sum_other], axis=1),
+        jnp.concatenate([sum_other, sum_half], axis=1),
     )
     stream_own = residual[0].astype(jnp.float32) + projected_sum
     stream = stream_own.astype(jnp.bfloat16)

time: 245 us -> 251 us (1.024)
  local copies, waits for them, and re-layouts: 12.5 us -> 16.5 us
  matrix products: 16.8 us -> 19.8 us
    all_gather x1, waiting for transfers between devices: 0.01 us -> 11.7 us  [per_device(): lax.all_gather(lax.dynamic_slice_in_dim(attn_proj, core * half_width, hal...]
    all_to_all x1, waiting for transfers between devices: 36.1 us -> 29.1 us  [per_device(): lax.all_to_all(token_minor, 'seq', split_axis=1, concat_axis=1, tiled=True)]
    all_to_all x1, waiting for transfers between devices: 16.4 us -> 12.8 us  [per_device(): lax.all_to_all(attended, 'seq', split_axis=0, concat_axis=2, tiled=True)]
    dot_general x1, matrix products: 1.99 us -> 5.33 us  [attend(): jnp.einsum('habce,chde->abhd', weights, values, preferred_element_type=jn...]
    unnamed x11 -> x17, local copies, waits for them, and re-layouts: 1.72 us -> 4.98 us
    all_gather x1, waiting for transfers between devices: 48.6 us -> 45.5 us  [per_device(): gathered = lax.all_gather(arrived, 'seq', axis=0, tiled=False)]
  transfers between devices with their start and end apart: 5 -> 6, of which waited for: 4 -> 5; matrix products, arithmetic and copies ran while one was open for 4% -> 5% of each run, Pallas kernels for 0% -> 0%
where the time goes in v6:
time: 251 us; the launch traced here: 250 us
  waiting for transfers between devices  151 us (60%)
  blocking collectives  33.5 us (13%)
  matrix products  19.8 us (8%)
  local copies, waits for them, and re-layouts  16.5 us (7%)
  between operations  13.3 us (5%)
  starting transfers between devices  12.7 us (5%)
  other arithmetic  3.65 us (1%)
    reduce_scatter x1, waiting for transfers between devices, per_device(): summed = lax.psum_scatter(pieces, 'seq', scatter_dimension=0, tiled=True)[0]  51.6 us
    all_gather x1, waiting for transfers between devices, per_device(): gathered = lax.all_gather(arrived, 'seq', axis=0, tiled=False)  45.5 us
    all_to_all x1, waiting for transfers between devices, per_device(): lax.all_to_all(token_minor, 'seq', split_axis=1, concat_axis=1, tiled=True)  29.1 us
    all_to_all x1, blocking collectives, per_device(): lax.all_to_all(dispatch, 'exp', split_axis=0, concat_axis=0, tiled=True)  17.1 us
    all_to_all x1, blocking collectives, per_device(): lax.all_to_all(summed, 'exp', split_axis=0, concat_axis=0, tiled=True)  16.5 us
    all_to_all x1, waiting for transfers between devices, per_device(): lax.all_to_all(attended, 'seq', split_axis=0, concat_axis=2, tiled=True)  12.8 us
    all_gather x1, waiting for transfers between devices, per_device(): lax.all_gather(lax.dynamic_slice_in_dim(attn_proj, core * half_width, hal...  11.7 us
    all_to_all x1, starting transfers between devices, per_device(): lax.all_to_all(token_minor, 'seq', split_axis=1, concat_axis=1, tiled=True)  8.47 us
  transfers between devices with their start and end apart: 6, of which 5 were waited for; matrix products, arithmetic and copies ran while one was open for 5% of the time, Pallas kernels for 0%

profile of v6, /device:TPU:8, one launch (start us, length us, event | category | flops | bytes accessed | tf_op | source)
XLA Modules:
  0.0 250.1 jit_solution(11451110571219415361)
XLA Ops:
  6.5 1.6 copy.22
  8.2 1.0 copy.23
  9.2 8.5 %all-to-all-start = ((bf16[3,8,160,128]{3,2,0,1:T(8,128)(2,1)}), bf16[3,8,160,128]{3,2,0,1:T(8,128)(2,1)S(1)}, u32[]{:S(2)}, u32[]{:S(2)}) async-start(bf16[3,8,160,128]{3,2,0,1:T(8,128)(2,1)} %copy.23), calls=%async_computation | async-start | bytes 1966080 | tf_op jit(solution)/shard_map/all_to_all | solution.py:51
  17.7 0.0 all-gather.4.cloned.1.call-start
  17.8 0.7 constant_dynamic-slice_fusion
  18.5 0.0 all-gather.4.cloned.1.call-update
  18.5 0.7 dynamic-slice_bitcast_fusion
  19.2 29.1 %all-to-all-done = bf16[3,8,160,128]{3,2,0,1:T(8,128)(2,1)S(1)} async-done(((bf16[3,8,160,128]{3,2,0,1:T(8,128)(2,1)}), bf16[3,8,160,128]{3,2,0,1:T(8,128)(2,1)S(1)}, u32[]{:S(2)}, u32[]{:S(2)}) %all-to-all-start) | async-done | bytes 983072 | tf_op jit(solution)/shard_map/all_to_all | solution.py:51
  48.2 0.1 fusion.52
  48.3 1.3 multiply_reduce_fusion
  49.6 3.2 %copy-done.1 = f32[2,8,128,8,128]{2,4,3,1,0:T(8,128)} copy-done((f32[2,8,128,8,128]{2,4,3,1,0:T(8,128)}, f32[2,8,128,8,128]{2,4,3,1,0:T(8,128)S(1)}, u32[]{:S(2)}) %copy-start.1) | copy-done | bytes 8388632
  52.8 1.4 fusion
  54.2 11.7 %all-gather.4.cloned.1.call-done = bf16[1280,640]{1,0:T(8,128)(2,1)} async-done(((bf16[160,640]{1,0:T(8,128)(2,1)}), bf16[1280,640]{1,0:T(8,128)(2,1)}) %all-gather.4.cloned.1.call-update) | async-done | bytes 1638416 | tf_op jit(solution)/shard_map/all_gather | solution.py:60
  65.9 0.0 collective-permute-start
  65.9 5.3 %fusion.23 = bf16[8,128,2,80]{1,3,0,2:T(8,128)(2,1)S(1)} fusion(f32[2,8,128,8,128]{2,4,3,1,0:T(8,128)} %copy-done.1, f32[2,8,128]{2,1,0:T(8,128)S(1)} %fusion, f32[2,8,128]{2,1,0:T(8,128)S(1)} %get-tuple-element.10, bf16[8,2,80,128,1]{3,2,1,0,4:T(8,128)(2,1)S(1)} %bitcast.131), kind=kOutput, calls=%fused_computation.31 | convolution fusion | flops 344096768 | bytes 9060352 | tf_op jit(solution)/shard_map/habce,chde->abhd/dot_general | solution.py:22
  71.3 0.8 copy.31
  72.0 3.9 %all-to-all-start.1 = ((bf16[8,128,1,160]{1,3,2,0:T(8,128)(2,1)}), bf16[8,128,1,160]{1,3,2,0:T(8,128)(2,1)S(1)}, u32[]{:S(2)}, u32[]{:S(2)}) async-start(bf16[8,128,1,160]{1,3,2,0:T(8,128)(2,1)} %bitcast.13), calls=%async_computation.1 | async-start | bytes 655360 | tf_op jit(solution)/shard_map/all_to_all | solution.py:54
  75.9 0.0 all-gather.6.cloned.1.call-start
  76.0 0.1 fusion.48
  76.1 0.2 reduce_window_sum.11
  76.2 0.2 select_reduce_fusion
  76.4 0.7 multiply_add_fusion.1
  77.1 12.8 %all-to-all-done.1 = bf16[8,128,1,160]{1,3,2,0:T(8,128)(2,1)S(1)} async-done(((bf16[8,128,1,160]{1,3,2,0:T(8,128)(2,1)}), bf16[8,128,1,160]{1,3,2,0:T(8,128)(2,1)S(1)}, u32[]{:S(2)}, u32[]{:S(2)}) %all-to-all-start.1) | async-done | bytes 327712 | tf_op jit(solution)/shard_map/all_to_all | solution.py:54
  89.9 0.5 fusion.53
  90.3 0.0 collective-permute-done
  90.4 1.9 fusion.54
  92.2 0.2 convert_reduce_fusion
  92.4 0.2 fusion.28
  92.7 0.4 convolution_convert_fusion.2
  93.1 0.4 copy.32
  93.5 17.1 %all_to_all.30 = bf16[8,2,12,1280]{3,1,2,0:T(2,128)(2,1)} all-to-all(bf16[8,2,12,1280]{3,1,2,0:T(2,128)(2,1)S(1)} %copy.32), channel_id=1, replica_groups=mesh['seq'=8,'exp'=8,'img'=4] {'exp'}, dimensions={0} | all-to-all | bytes 983040 | tf_op jit(solution)/shard_map/all_to_all | solution.py:90
  110.6 0.0 all-gather.6.cloned.1.call-update
  110.6 0.2 reduce-scatter.2.cloned.1.call-start
  110.8 45.5 %all-gather.6.cloned.1.call-done = bf16[64,2,12,1280]{3,1,2,0:T(2,128)(2,1)} async-done(((bf16[8,2,12,1280]{3,1,2,0:T(2,128)(2,1)}), bf16[64,2,12,1280]{3,1,2,0:T(2,128)(2,1)}) %all-gather.6.cloned.1.call-update) | async-done | bytes 3932176 | tf_op jit(solution)/shard_map/all_gather | solution.py:91
  156.3 3.0 %copy.33 = bf16[64,2,12,1280]{3,2,0,1:T(8,128)(2,1)S(1)} copy(bf16[64,2,12,1280]{3,1,2,0:T(2,128)(2,1)} %all-gather.6.cloned.1.call-done) | data formatting | bytes 7864320 | tf_op jit(solution)/shard_map/all_gather | solution.py:91
  159.3 0.1 copy-done.4
  159.4 2.4 multiply_convert_fusion
  161.9 0.0 copy-start.5
  161.9 2.4 multiply_convert_fusion.1
  164.3 2.2 fusion.3
  166.5 2.2 fusion.2
  168.8 0.7 pad_maximum_fusion
  169.5 3.4 %copy.34 = bf16[8,8,2,12,1280]{4,1,3,2,0:T(8,128)(2,1)} copy(bf16[8,8,2,12,1280]{4,3,1,0,2:T(8,128)(2,1)S(1)} %pad_maximum_fusion) | data formatting | bytes 7864320 | tf_op jit(solution)/shard_map/stack | solution.py:106
  172.9 0.0 reduce-scatter.2.cloned.1.call-update
  172.9 51.6 %reduce-scatter.2.cloned.1.call-done = bf16[1,8,2,12,1280]{4,1,3,2,0:T(8,128)(2,1)} async-done(((bf16[8,8,2,12,1280]{4,1,3,2,0:T(8,128)(2,1)}), bf16[1,8,2,12,1280]{4,1,3,2,0:T(8,128)(2,1)}) %reduce-scatter.2.cloned.1.call-update) | async-done | bytes 491536 | tf_op jit(solution)/shard_map/reduce_scatter | solution.py:107
  224.5 1.5 copy.35
  226.0 16.5 %all_to_all.31 = bf16[8,2,12,1280]{3,1,2,0:T(2,128)(2,1)S(1)} all-to-all(bf16[8,2,12,1280]{3,1,2,0:T(2,128)(2,1)S(1)} %copy.35), channel_id=1, replica_groups=mesh['seq'=8,'exp'=8,'img'=4] {'exp'}, dimensions={0} | all-to-all | bytes 983040 | tf_op jit(solution)/shard_map/all_to_all | solution.py:108
  242.5 1.1 fusion.8
  (16 shorter events, 0.0 us)
Async XLA Ops:
  6.5 11.2 %copy-start = (bf16[160,1280]{1,0:T(8,128)(2,1)S(1)}, bf16[160,1280]{1,0:T(8,128)(2,1)}, u32[]{:S(2)}) copy-start(bf16[160,1280]{1,0:T(8,128)(2,1)} %param.10) | copy-start | bytes 1228804
  9.2 39.0 %all-to-all-start = ((bf16[3,8,160,128]{3,2,0,1:T(8,128)(2,1)}), bf16[3,8,160,128]{3,2,0,1:T(8,128)(2,1)S(1)}, u32[]{:S(2)}, u32[]{:S(2)}) async-start(bf16[3,8,160,128]{3,2,0,1:T(8,128)(2,1)} %copy.23), calls=%async_computation | async-start | bytes 1966080 | tf_op jit(solution)/shard_map/all_to_all | solution.py:51
  17.7 48.3 %all-gather.4.cloned.1.call-start = ((), (), s32[]{:S(2)}) async-start(), calls=%async_computation.5 | async-start | bytes 1843200 | tf_op jit(solution)/shard_map/all_gather | solution.py:60
  49.6 3.2 %copy-start.1 = (f32[2,8,128,8,128]{2,4,3,1,0:T(8,128)}, f32[2,8,128,8,128]{2,4,3,1,0:T(8,128)S(1)}, u32[]{:S(2)}) copy-start(f32[2,8,128,8,128]{2,4,3,1,0:T(8,128)S(1)} %get-tuple-element.11) | copy-start | bytes 25165828
  65.9 24.4 %collective-permute-start = (bf16[1280,640]{1,0:T(8,128)(2,1)}, bf16[1280,640]{1,0:T(8,128)(2,1)}, u32[]{:S(2)}, u32[]{:S(2)}) collective-permute-start(bf16[1280,640]{1,0:T(8,128)(2,1)} %all-gather.4.cloned.1.call-done), channel_id=1, source_target_pairs={{0,1},{1,0},{2,3},{3,2},{4,5},{5,4},{6,7},{7,6},{8,9},{9,8},{10,11... | collective-permute-start | bytes 4915208 | tf_op jit(solution)/shard_map/ppermute | solution.py:66
  65.9 23.9 %copy-start.2 = (bf16[1280,640]{1,0:T(8,128)(2,1)S(1)}, bf16[1280,640]{1,0:T(8,128)(2,1)}, u32[]{:S(2)}) copy-start(bf16[1280,640]{1,0:T(8,128)(2,1)} %all-gather.4.cloned.1.call-done) | copy-start | bytes 4915204
  72.0 20.2 %copy-start.3 = (bf16[1,128,1280]{2,1,0:T(8,128)(2,1)S(1)}, bf16[1,128,1280]{2,1,0:T(8,128)(2,1)}, u32[]{:S(2)}) copy-start(bf16[1,128,1280]{2,1,0:T(8,128)(2,1)} %param.9) | copy-start | bytes 983044
  72.0 17.8 %all-to-all-start.1 = ((bf16[8,128,1,160]{1,3,2,0:T(8,128)(2,1)}), bf16[8,128,1,160]{1,3,2,0:T(8,128)(2,1)S(1)}, u32[]{:S(2)}, u32[]{:S(2)}) async-start(bf16[8,128,1,160]{1,3,2,0:T(8,128)(2,1)} %bitcast.13), calls=%async_computation.1 | async-start | bytes 655360 | tf_op jit(solution)/shard_map/all_to_all | solution.py:54
  75.9 80.4 %all-gather.6.cloned.1.call-start = ((), (), s32[]{:S(2)}) async-start(), calls=%async_computation.7 | async-start | bytes 4423680 | tf_op jit(solution)/shard_map/all_gather | solution.py:91
  89.9 2.8 %copy-start.6 = (f32[1280]{0:T(1024)S(1)}, f32[1280]{0:T(1024)}, u32[]{:S(2)}) copy-start(f32[1280]{0:T(1024)} %param.12) | copy-start | bytes 15364
  89.9 2.8 %copy-start.7 = (f32[1280]{0:T(1024)S(1)}, f32[1280]{0:T(1024)}, u32[]{:S(2)}) copy-start(f32[1280]{0:T(1024)} %param.11) | copy-start | bytes 15364
  110.6 113.9 %reduce-scatter.2.cloned.1.call-start = ((), (), s32[]{:S(2)}) async-start(), calls=%async_computation.6 | async-start | bytes 4423680 | tf_op jit(solution)/shard_map/reduce_scatter | solution.py:107
  156.3 3.1 %copy-start.4 = (bf16[2,1280,640]{2,1,0:T(8,128)(2,1)S(1)}, bf16[2,1280,640]{2,1,0:T(8,128)(2,1)}, u32[]{:S(2)}) copy-start(bf16[2,1280,640]{2,1,0:T(8,128)(2,1)} %param.14) | copy-start | bytes 9830404
  161.9 2.5 copy-start.5
Sparse Core Ops, SparseCore 0:
  20.3 45.6 all-gather.3
  110.7 45.5 all-gather.5
  173.0 51.4 reduce-scatter.1

commit v7 on v5

--- a/solution.py
+++ b/solution.py
@@ -18,7 +18,7 @@
     )
     peak = jnp.max(scores, axis=(3, 4), keepdims=True)
     powers = jnp.exp(scores - peak)
-    weights = (powers / jnp.sum(powers, axis=(3, 4), keepdims=True)).astype(jnp.bfloat16)
+    weights = (powers * (1.0 / jnp.sum(powers, axis=(3, 4), keepdims=True))).astype(jnp.bfloat16)
     mixed = jnp.einsum("habce,chde->abhd", weights, values, preferred_element_type=jnp.float32)
     return mixed.astype(jnp.bfloat16)
 
@@ -28,7 +28,7 @@
     centre = jnp.mean(values, axis=-1, keepdims=True)
     centered = values - centre
     variance = jnp.mean(centered * centered, axis=-1, keepdims=True)
-    return (centered / jnp.sqrt(variance + 1e-06) * norm_gain + norm_bias).astype(jnp.bfloat16)
+    return (centered * lax.rsqrt(variance + 1e-06) * norm_gain + norm_bias).astype(jnp.bfloat16)
 
 
 def per_device(

time: 245 us -> 245 us (level)
  no operation moved by 1% of the time
where the time goes in v7:
time: 245 us; the launch traced here: 244 us
  waiting for transfers between devices  153 us (62%)
  blocking collectives  32.9 us (13%)
  matrix products  16.6 us (7%)
  between operations  13.3 us (5%)
  local copies, waits for them, and re-layouts  12.5 us (5%)
  starting transfers between devices  12.2 us (5%)
  other arithmetic  3.42 us (1%)
    reduce_scatter x1, waiting for transfers between devices, per_device(): summed = lax.psum_scatter(pieces, 'seq', scatter_dimension=0, tiled=True)[0]  51.6 us
    all_gather x1, waiting for transfers between devices, per_device(): gathered = lax.all_gather(arrived, 'seq', axis=0, tiled=False)  48.6 us
    all_to_all x1, waiting for transfers between devices, per_device(): lax.all_to_all(token_minor, 'seq', split_axis=1, concat_axis=1, tiled=True)  36.1 us
    all_to_all x1, blocking collectives, per_device(): lax.all_to_all(summed, 'exp', split_axis=0, concat_axis=0, tiled=True)  16.5 us
    all_to_all x1, blocking collectives, per_device(): lax.all_to_all(dispatch, 'exp', split_axis=0, concat_axis=0, tiled=True)  16.5 us
    all_to_all x1, waiting for transfers between devices, per_device(): lax.all_to_all(attended, 'seq', split_axis=0, concat_axis=2, tiled=True)  16.4 us
    all_to_all x1, starting transfers between devices, per_device(): lax.all_to_all(token_minor, 'seq', split_axis=1, concat_axis=1, tiled=True)  8.47 us
  transfers between devices with their start and end apart: 5, of which 4 were waited for; matrix products, arithmetic and copies ran while one was open for 4% of the time, Pallas kernels for 0%

profile of v7, /device:TPU:8, one launch (start us, length us, event | category | flops | bytes accessed | tf_op | source)
XLA Modules:
  0.0 244.4 jit_solution(5946868216613501484)
XLA Ops:
  6.5 0.0 all-gather.4.cloned.1.call-start
  6.5 0.7 all-gather.4.cloned.1.call-update
  7.3 1.6 copy.22
  8.9 1.0 copy.23
  9.9 8.5 %all-to-all-start = ((bf16[3,8,160,128]{3,2,0,1:T(8,128)(2,1)}), bf16[3,8,160,128]{3,2,0,1:T(8,128)(2,1)S(1)}, u32[]{:S(2)}, u32[]{:S(2)}) async-start(bf16[3,8,160,128]{3,2,0,1:T(8,128)(2,1)} %copy.23), calls=%async_computation | async-start | bytes 1966080 | tf_op jit(solution)/shard_map/all_to_all | solution.py:51
  18.4 0.7 dynamic-slice_bitcast_fusion
  19.0 36.1 %all-to-all-done = bf16[3,8,160,128]{3,2,0,1:T(8,128)(2,1)S(1)} async-done(((bf16[3,8,160,128]{3,2,0,1:T(8,128)(2,1)}), bf16[3,8,160,128]{3,2,0,1:T(8,128)(2,1)S(1)}, u32[]{:S(2)}, u32[]{:S(2)}) %all-to-all-start) | async-done | bytes 983072 | tf_op jit(solution)/shard_map/all_to_all | solution.py:51
  55.1 0.1 fusion.45
  55.2 1.3 multiply_reduce_fusion
  56.5 1.4 fusion
  57.9 0.0 copy-start
  57.9 1.8 fusion.25
  59.7 0.0 copy-start.1
  59.7 0.0 copy-start.2
  59.7 0.7 copy.31
  60.5 3.4 %all-to-all-start.1 = ((bf16[8,128,1,160]{1,3,2,0:T(8,128)(2,1)}), bf16[8,128,1,160]{1,3,2,0:T(8,128)(2,1)S(1)}, u32[]{:S(2)}, u32[]{:S(2)}) async-start(bf16[8,128,1,160]{1,3,2,0:T(8,128)(2,1)} %bitcast.13), calls=%async_computation.1 | async-start | bytes 655360 | tf_op jit(solution)/shard_map/all_to_all | solution.py:54
  63.9 0.0 all-gather.6.cloned.1.call-start
  64.0 0.1 fusion.43
  64.1 0.2 reduce_window_sum.11
  64.2 0.2 select_reduce_fusion
  64.4 0.7 multiply_add_fusion.1
  65.1 16.4 %all-to-all-done.1 = bf16[8,128,1,160]{1,3,2,0:T(8,128)(2,1)S(1)} async-done(((bf16[8,128,1,160]{1,3,2,0:T(8,128)(2,1)}), bf16[8,128,1,160]{1,3,2,0:T(8,128)(2,1)S(1)}, u32[]{:S(2)}, u32[]{:S(2)}) %all-to-all-start.1) | async-done | bytes 327712 | tf_op jit(solution)/shard_map/all_to_all | solution.py:54
  81.5 0.0 copy-done
  81.5 2.6 %fusion.46 = (f32[128]{0:T(128)S(1)}, f32[128,1280]{1,0:T(8,128)S(1)}) fusion(bf16[128,1280]{0,1:T(8,128)(2,1)S(1)} %bitcast.114, bf16[1280,1280]{1,0:T(8,128)(2,1)} %all-gather.4.cloned.1.call-done, bf16[1,128,1280]{2,1,0:T(8,128)(2,1)S(1)} %copy-done), kind=kOutput, calls=%fused_computation.64 | convolution fusion | flops 420249472 | bytes 4588032 | tf_op jit(solution)/shard_map/dot_general | solution.py:57
  84.1 0.2 multiply_reduce_fusion.1
  84.4 0.0 copy-done.1
  84.4 0.0 copy-done.2
  84.4 0.4 convolution_convert_fusion.2
  84.8 0.4 copy.32
  85.2 16.5 %all_to_all.30 = bf16[8,2,12,1280]{3,1,2,0:T(2,128)(2,1)} all-to-all(bf16[8,2,12,1280]{3,1,2,0:T(2,128)(2,1)S(1)} %copy.32), channel_id=1, replica_groups=mesh['seq'=8,'exp'=8,'img'=4] {'exp'}, dimensions={0} | all-to-all | bytes 983040 | tf_op jit(solution)/shard_map/all_to_all | solution.py:78
  101.7 0.0 all-gather.6.cloned.1.call-update
  101.7 0.2 reduce-scatter.2.cloned.1.call-start
  101.9 48.6 %all-gather.6.cloned.1.call-done = bf16[64,2,12,1280]{3,1,2,0:T(2,128)(2,1)} async-done(((bf16[8,2,12,1280]{3,1,2,0:T(2,128)(2,1)}), bf16[64,2,12,1280]{3,1,2,0:T(2,128)(2,1)}) %all-gather.6.cloned.1.call-update) | async-done | bytes 3932176 | tf_op jit(solution)/shard_map/all_gather | solution.py:79
  150.5 3.0 %copy.33 = bf16[64,2,12,1280]{3,2,0,1:T(8,128)(2,1)S(1)} copy(bf16[64,2,12,1280]{3,1,2,0:T(2,128)(2,1)} %all-gather.6.cloned.1.call-done) | data formatting | bytes 7864320 | tf_op jit(solution)/shard_map/all_gather | solution.py:79
  153.5 0.1 copy-done.3
  153.6 2.4 multiply_convert_fusion.3
  156.1 0.0 copy-start.4
  156.1 2.4 multiply_convert_fusion.2
  158.5 0.0 copy-done.4
  158.5 2.2 fusion.2
  160.8 2.2 fusion.3
  163.0 0.7 pad_maximum_fusion
  163.7 3.4 %copy.34 = bf16[8,8,2,12,1280]{4,1,3,2,0:T(8,128)(2,1)} copy(bf16[8,8,2,12,1280]{4,3,1,0,2:T(8,128)(2,1)S(1)} %pad_maximum_fusion) | data formatting | bytes 7864320 | tf_op jit(solution)/shard_map/stack | solution.py:94
  167.1 0.0 reduce-scatter.2.cloned.1.call-update
  167.1 51.6 %reduce-scatter.2.cloned.1.call-done = bf16[1,8,2,12,1280]{4,1,3,2,0:T(8,128)(2,1)} async-done(((bf16[8,8,2,12,1280]{4,1,3,2,0:T(8,128)(2,1)}), bf16[1,8,2,12,1280]{4,1,3,2,0:T(8,128)(2,1)}) %reduce-scatter.2.cloned.1.call-update) | async-done | bytes 491536 | tf_op jit(solution)/shard_map/reduce_scatter | solution.py:95
  218.7 1.5 copy.35
  220.2 16.5 %all_to_all.31 = bf16[8,2,12,1280]{3,1,2,0:T(2,128)(2,1)S(1)} all-to-all(bf16[8,2,12,1280]{3,1,2,0:T(2,128)(2,1)S(1)} %copy.35), channel_id=1, replica_groups=mesh['seq'=8,'exp'=8,'img'=4] {'exp'}, dimensions={0} | all-to-all | bytes 983040 | tf_op jit(solution)/shard_map/all_to_all | solution.py:96
  236.7 1.1 fusion.10
  (6 shorter events, 0.0 us)
Async XLA Ops:
  6.5 74.9 %all-gather.4.cloned.1.call-start = ((), (), s32[]{:S(2)}) async-start(), calls=%async_computation.5 | async-start | bytes 3686400 | tf_op jit(solution)/shard_map/all_gather | solution.py:59
  9.9 45.2 %all-to-all-start = ((bf16[3,8,160,128]{3,2,0,1:T(8,128)(2,1)}), bf16[3,8,160,128]{3,2,0,1:T(8,128)(2,1)S(1)}, u32[]{:S(2)}, u32[]{:S(2)}) async-start(bf16[3,8,160,128]{3,2,0,1:T(8,128)(2,1)} %copy.23), calls=%async_computation | async-start | bytes 1966080 | tf_op jit(solution)/shard_map/all_to_all | solution.py:51
  57.9 23.6 %copy-start = (bf16[1,128,1280]{2,1,0:T(8,128)(2,1)S(1)}, bf16[1,128,1280]{2,1,0:T(8,128)(2,1)}, u32[]{:S(2)}) copy-start(bf16[1,128,1280]{2,1,0:T(8,128)(2,1)} %param.9) | copy-start | bytes 983044
  59.7 24.7 %copy-start.1 = (f32[1280]{0:T(1024)S(1)}, f32[1280]{0:T(1024)}, u32[]{:S(2)}) copy-start(f32[1280]{0:T(1024)} %param.12) | copy-start | bytes 15364
  59.7 24.7 %copy-start.2 = (f32[1280]{0:T(1024)S(1)}, f32[1280]{0:T(1024)}, u32[]{:S(2)}) copy-start(f32[1280]{0:T(1024)} %param.11) | copy-start | bytes 15364
  60.5 21.0 %all-to-all-start.1 = ((bf16[8,128,1,160]{1,3,2,0:T(8,128)(2,1)}), bf16[8,128,1,160]{1,3,2,0:T(8,128)(2,1)S(1)}, u32[]{:S(2)}, u32[]{:S(2)}) async-start(bf16[8,128,1,160]{1,3,2,0:T(8,128)(2,1)} %bitcast.13), calls=%async_computation.1 | async-start | bytes 655360 | tf_op jit(solution)/shard_map/all_to_all | solution.py:54
  63.9 86.6 %all-gather.6.cloned.1.call-start = ((), (), s32[]{:S(2)}) async-start(), calls=%async_computation.7 | async-start | bytes 4423680 | tf_op jit(solution)/shard_map/all_gather | solution.py:79
  101.7 117.0 %reduce-scatter.2.cloned.1.call-start = ((), (), s32[]{:S(2)}) async-start(), calls=%async_computation.6 | async-start | bytes 4423680 | tf_op jit(solution)/shard_map/reduce_scatter | solution.py:95
  150.5 3.1 %copy-start.3 = (bf16[2,1280,640]{2,1,0:T(8,128)(2,1)S(1)}, bf16[2,1280,640]{2,1,0:T(8,128)(2,1)}, u32[]{:S(2)}) copy-start(bf16[2,1280,640]{2,1,0:T(8,128)(2,1)} %param.14) | copy-start | bytes 9830404
  156.1 2.5 %copy-start.4 = (bf16[2,640,1280]{2,1,0:T(8,128)(2,1)S(1)}, bf16[2,640,1280]{2,1,0:T(8,128)(2,1)}, u32[]{:S(2)}) copy-start(bf16[2,640,1280]{2,1,0:T(8,128)(2,1)} %param.15) | copy-start | bytes 9830404
Sparse Core Ops, SparseCore 0:
  9.1 71.9 all-gather.3
  101.8 48.6 all-gather.5
  167.2 51.4 reduce-scatter.1

commit v8 on v7

--- a/solution.py
+++ b/solution.py
@@ -77,21 +77,18 @@
     ).astype(jnp.bfloat16)
     arrived = lax.all_to_all(dispatch, "exp", split_axis=0, concat_axis=0, tiled=True)
     gathered = lax.all_gather(arrived, "seq", axis=0, tiled=False)
-    pieces = []
-    for local in range(local_experts):
-        lifted = jnp.einsum(
-            "secd,df->secf",
-            gathered[:, :, local],
-            expert_up[local],
-            preferred_element_type=jnp.float32,
-        )
-        hidden = (0.5 * lifted * (1.0 + lax.erf(lifted * (0.5**0.5)))).astype(jnp.bfloat16)
-        hidden = lax.optimization_barrier(hidden)
-        piece = jnp.einsum(
-            "secf,fd->secd", hidden, expert_down[local], preferred_element_type=jnp.float32
-        )
-        pieces.append(piece.astype(jnp.bfloat16))
-    pieces = jnp.stack(pieces, axis=2)
+    hid_local = expert_up.shape[2]
+    rows = gathered.reshape(-1, model_width)
+    up_both = jnp.transpose(expert_up, (1, 0, 2)).reshape(model_width, local_experts * hid_local)
+    lifted = jnp.dot(rows, up_both, preferred_element_type=jnp.float32)
+    row_expert = (jnp.arange(rows.shape[0], dtype=jnp.int32) // cap_dev) % local_experts
+    col_expert = jnp.arange(local_experts * hid_local, dtype=jnp.int32) // hid_local
+    own = row_expert[:, None] == col_expert[None, :]
+    activated = 0.5 * lifted * (1.0 + lax.erf(lifted * (0.5**0.5)))
+    hidden = lax.optimization_barrier(jnp.where(own, activated, 0.0).astype(jnp.bfloat16))
+    down_both = expert_down.reshape(local_experts * hid_local, model_width)
+    pieces = jnp.dot(hidden, down_both, preferred_element_type=jnp.float32).astype(jnp.bfloat16)
+    pieces = pieces.reshape(gathered.shape)
     summed = lax.psum_scatter(pieces, "seq", scatter_dimension=0, tiled=True)[0]
     returned = lax.all_to_all(summed, "exp", split_axis=0, concat_axis=0, tiled=True)
     expert_out = jnp.einsum(

time: 245 us -> 279 us (1.14)
  local copies, waits for them, and re-layouts: 12.5 us -> 35 us
  matrix products: 16.6 us -> 24 us
  waiting for transfers between devices: 153 us -> 157 us
    reshape x0 -> x2, local copies, waits for them, and re-layouts: none -> 14 us  [the longest x1 7.07 us: per_device(): rows = gathered.reshape(-1, model_width)]
    reduce_scatter x1, waiting for transfers between devices: 51.6 us -> 64 us  [per_device(): summed = lax.psum_scatter(pieces, 'seq', scatter_dimension=0, tiled=True)[0]]
    all_gather x1, waiting for transfers between devices: 48.6 us -> 39.8 us  [per_device(): gathered = lax.all_gather(arrived, 'seq', axis=0, tiled=False)]
    unnamed x11 -> x10, local copies, waits for them, and re-layouts: 1.72 us -> 8.78 us
    dot_general x4 -> x2, matrix products: 9.27 us -> 15.5 us  [the longest x1 8.67 us: per_device(): lifted = jnp.dot(rows, up_both, preferred_element_type=jnp.float32)]
    another operation x1 -> x0, local copies, waits for them, and re-layouts: 3.39 us -> none  [per_device(): pieces = jnp.stack(pieces, axis=2)]
  transfers between devices with their start and end apart: 5 -> 5, of which waited for: 4 -> 4; matrix products, arithmetic and copies ran while one was open for 4% -> 7% of each run, Pallas kernels for 0% -> 0%
where the time goes in v8:
time: 279 us
  waiting for transfers between devices  157 us (56%)
  local copies, waits for them, and re-layouts  35 us (13%)
  blocking collectives  33.4 us (12%)
  matrix products  24 us (9%)
  between operations  13.2 us (5%)
  starting transfers between devices  12.8 us (5%)
    reduce_scatter x1, waiting for transfers between devices, per_device(): summed = lax.psum_scatter(pieces, 'seq', scatter_dimension=0, tiled=True)[0]  64 us
    all_gather x1, waiting for transfers between devices, per_device(): gathered = lax.all_gather(arrived, 'seq', axis=0, tiled=False)  39.8 us
    all_to_all x1, waiting for transfers between devices, per_device(): lax.all_to_all(token_minor, 'seq', split_axis=1, concat_axis=1, tiled=True)  37.3 us
    all_to_all x1, blocking collectives, per_device(): lax.all_to_all(dispatch, 'exp', split_axis=0, concat_axis=0, tiled=True)  16.9 us
    all_to_all x1, blocking collectives, per_device(): lax.all_to_all(summed, 'exp', split_axis=0, concat_axis=0, tiled=True)  16.5 us
    all_to_all x1, waiting for transfers between devices, per_device(): lax.all_to_all(attended, 'seq', split_axis=0, concat_axis=2, tiled=True)  15.4 us
    unnamed x10, local copies, waits for them, and re-layouts  8.78 us
    dot_general x1, matrix products, per_device(): lifted = jnp.dot(rows, up_both, preferred_element_type=jnp.float32)  8.67 us
  transfers between devices with their start and end apart: 5, of which 4 were waited for; matrix products, arithmetic and copies ran while one was open for 7% of the time, Pallas kernels for 0%

profile of v8, /device:TPU:8, one launch (start us, length us, event | category | flops | bytes accessed | tf_op | source)
XLA Modules:
  0.0 278.5 jit_solution(14648194568745348632)
XLA Ops:
  6.5 0.0 copy-start
  6.5 0.0 all-gather.4.cloned.1.call-start
  6.5 0.7 all-gather.4.cloned.1.call-update
  7.3 2.5 copy.17
  9.8 2.2 copy.18
  12.0 8.5 %all-to-all-start = ((bf16[3,8,160,128]{3,2,0,1:T(8,128)(2,1)}), bf16[3,8,160,128]{3,2,0,1:T(8,128)(2,1)}, u32[]{:S(2)}, u32[]{:S(2)}) async-start(bf16[3,8,160,128]{3,2,0,1:T(8,128)(2,1)} %copy.18), calls=%async_computation | async-start | bytes 1966080 | tf_op jit(solution)/shard_map/all_to_all | solution.py:51
  20.5 0.7 dynamic-slice_bitcast_fusion
  21.1 37.3 %all-to-all-done = bf16[3,8,160,128]{3,2,0,1:T(8,128)(2,1)} async-done(((bf16[3,8,160,128]{3,2,0,1:T(8,128)(2,1)}), bf16[3,8,160,128]{3,2,0,1:T(8,128)(2,1)}, u32[]{:S(2)}, u32[]{:S(2)}) %all-to-all-start) | async-done | bytes 983072 | tf_op jit(solution)/shard_map/all_to_all | solution.py:51
  58.4 1.2 fusion.36
  59.7 1.3 multiply_reduce_fusion
  61.0 1.4 fusion
  62.4 0.0 copy-start.2
  62.4 0.0 copy-start.3
  62.4 1.8 fusion.9
  64.2 0.8 copy.26
  65.0 4.1 %all-to-all-start.1 = ((bf16[8,128,1,160]{1,3,2,0:T(8,128)(2,1)}), bf16[8,128,1,160]{1,3,2,0:T(8,128)(2,1)}, u32[]{:S(2)}, u32[]{:S(2)}) async-start(bf16[8,128,1,160]{1,3,2,0:T(8,128)(2,1)} %bitcast.75), calls=%async_computation.1 | async-start | bytes 655360 | tf_op jit(solution)/shard_map/all_to_all | solution.py:54
  69.1 0.0 all-gather.6.cloned.1.call-start
  69.1 0.1 fusion.27
  69.2 0.2 reduce_window_sum.11
  69.4 0.2 select_reduce_fusion
  69.6 0.7 multiply_add_fusion.1
  70.2 15.4 %all-to-all-done.1 = bf16[8,128,1,160]{1,3,2,0:T(8,128)(2,1)} async-done(((bf16[8,128,1,160]{1,3,2,0:T(8,128)(2,1)}), bf16[8,128,1,160]{1,3,2,0:T(8,128)(2,1)}, u32[]{:S(2)}, u32[]{:S(2)}) %all-to-all-start.1) | async-done | bytes 327712 | tf_op jit(solution)/shard_map/all_to_all | solution.py:54
  85.6 0.0 all-gather.4.cloned.1.call-done
  85.6 2.8 fusion.37
  88.4 0.0 copy-start.1
  88.4 0.2 multiply_reduce_fusion.1
  88.7 0.6 copy-done.1
  89.3 0.0 copy-done.2
  89.3 0.0 copy-done.3
  89.3 0.4 convolution_convert_fusion.1
  89.7 0.4 copy.27
  90.1 16.9 %all_to_all.30 = bf16[8,2,12,1280]{3,1,2,0:T(2,128)(2,1)} all-to-all(bf16[8,2,12,1280]{3,1,2,0:T(2,128)(2,1)S(1)} %copy.27), channel_id=1, replica_groups=mesh['seq'=8,'exp'=8,'img'=4] {'exp'}, dimensions={0} | all-to-all | bytes 983040 | tf_op jit(solution)/shard_map/all_to_all | solution.py:78
  107.1 0.0 all-gather.6.cloned.1.call-update
  107.1 0.2 reduce-scatter.2.cloned.1.call-start
  107.3 5.6 %copy.29 = bf16[2,1280,640]{1,2,0:T(8,128)(2,1)} copy(bf16[2,1280,640]{2,1,0:T(8,128)(2,1)} %param.14) | data formatting | bytes 6553600 | tf_op args[6]
  113.0 39.8 %all-gather.6.cloned.1.call-done = bf16[64,2,12,1280]{3,1,2,0:T(2,128)(2,1)} async-done(((bf16[8,2,12,1280]{3,1,2,0:T(2,128)(2,1)}), bf16[64,2,12,1280]{3,1,2,0:T(2,128)(2,1)}) %all-gather.6.cloned.1.call-update) | async-done | bytes 3932176 | tf_op jit(solution)/shard_map/all_gather | solution.py:79
  152.8 5.5 %copy.28 = bf16[64,2,12,1280]{3,2,1,0:T(8,128)(2,1)} copy(bf16[64,2,12,1280]{3,1,2,0:T(2,128)(2,1)} %all-gather.6.cloned.1.call-done) | data formatting | bytes 7864320 | tf_op jit(solution)/shard_map/all_gather | solution.py:79
  158.3 7.1 %reshape.120 = bf16[1536,1280]{1,0:T(8,128)(2,1)} reshape(bf16[64,2,12,1280]{3,2,1,0:T(8,128)(2,1)} %copy.28) | data formatting | bytes 7864320 | tf_op jit(solution)/shard_map/reshape | solution.py:81
  165.4 8.7 %select_convert_fusion = bf16[1536,1280]{1,0:T(8,128)(2,1)S(1)} fusion(s32[1280]{0:T(1024)S(1)} %add_select_fusion, s32[1536]{0:T(1024)S(1)} %add_select_fusion.1, bf16[1536,1280]{1,0:T(8,128)(2,1)} %reshape.120, bf16[1280,1280]{0,1:T(8,128)(2,1)} %bitcast.72), kind=kOutput, calls=%fused_computation.3 | convolution fusion | flops 5046927360 | bytes 11152384 | tf_op jit(solution)/shard_map/dot_general | solution.py:83
  174.1 0.0 copy-done
  174.1 6.8 %convolution_convert_fusion = bf16[1536,1280]{1,0:T(8,128)(2,1)} fusion(bf16[1536,1280]{1,0:T(8,128)(2,1)S(1)} %select_convert_fusion, bf16[1280,1280]{1,0:T(8,128)(2,1)S(1)} %bitcast.70), kind=kOutput, calls=%fused_computation.4 | convolution fusion | flops 5035130880 | bytes 11141120 | tf_op jit(solution)/shard_map/dot_general | solution.py:90
  180.9 6.9 %reshape.123 = bf16[8,8,2,12,1280]{4,3,2,1,0:T(8,128)(2,1)} reshape(bf16[1536,1280]{1,0:T(8,128)(2,1)} %convolution_convert_fusion) | data formatting | bytes 7864320 | tf_op jit(solution)/shard_map/reshape | solution.py:91
  187.9 0.0 reduce-scatter.2.cloned.1.call-update
  187.9 64.0 %reduce-scatter.2.cloned.1.call-done = bf16[1,8,2,12,1280]{4,3,2,1,0:T(8,128)(2,1)} async-done(((bf16[8,8,2,12,1280]{4,3,2,1,0:T(8,128)(2,1)}), bf16[1,8,2,12,1280]{4,3,2,1,0:T(8,128)(2,1)}) %reduce-scatter.2.cloned.1.call-update) | async-done | bytes 491536 | tf_op jit(solution)/shard_map/reduce_scatter | solution.py:92
  251.9 1.5 copy.30
  253.3 16.5 %all_to_all.31 = bf16[8,2,12,1280]{3,1,2,0:T(2,128)(2,1)S(1)} all-to-all(bf16[8,2,12,1280]{3,1,2,0:T(2,128)(2,1)S(1)} %copy.30), channel_id=1, replica_groups=mesh['seq'=8,'exp'=8,'img'=4] {'exp'}, dimensions={0} | all-to-all | bytes 983040 | tf_op jit(solution)/shard_map/all_to_all | solution.py:93
  269.8 2.2 fusion.6
  (6 shorter events, 0.1 us)
Async XLA Ops:
  6.5 167.6 %copy-start = (bf16[2,640,1280]{2,1,0:T(8,128)(2,1)S(1)}, bf16[2,640,1280]{2,1,0:T(8,128)(2,1)}, u32[]{:S(2)}) copy-start(bf16[2,640,1280]{2,1,0:T(8,128)(2,1)} %param.15) | copy-start | bytes 9830404
  6.5 79.1 %all-gather.4.cloned.1.call-start = ((), (), s32[]{:S(2)}) async-start(), calls=%async_computation.5 | async-start | bytes 3686400 | tf_op jit(solution)/shard_map/all_gather | solution.py:59
  12.0 46.4 %all-to-all-start = ((bf16[3,8,160,128]{3,2,0,1:T(8,128)(2,1)}), bf16[3,8,160,128]{3,2,0,1:T(8,128)(2,1)}, u32[]{:S(2)}, u32[]{:S(2)}) async-start(bf16[3,8,160,128]{3,2,0,1:T(8,128)(2,1)} %copy.18), calls=%async_computation | async-start | bytes 1966080 | tf_op jit(solution)/shard_map/all_to_all | solution.py:51
  62.4 26.9 %copy-start.2 = (f32[1280]{0:T(1024)S(1)}, f32[1280]{0:T(1024)}, u32[]{:S(2)}) copy-start(f32[1280]{0:T(1024)} %param.12) | copy-start | bytes 15364
  62.4 26.9 %copy-start.3 = (f32[1280]{0:T(1024)S(1)}, f32[1280]{0:T(1024)}, u32[]{:S(2)}) copy-start(f32[1280]{0:T(1024)} %param.11) | copy-start | bytes 15364
  65.0 20.7 %all-to-all-start.1 = ((bf16[8,128,1,160]{1,3,2,0:T(8,128)(2,1)}), bf16[8,128,1,160]{1,3,2,0:T(8,128)(2,1)}, u32[]{:S(2)}, u32[]{:S(2)}) async-start(bf16[8,128,1,160]{1,3,2,0:T(8,128)(2,1)} %bitcast.75), calls=%async_computation.1 | async-start | bytes 655360 | tf_op jit(solution)/shard_map/all_to_all | solution.py:54
  69.1 83.7 %all-gather.6.cloned.1.call-start = ((), (), s32[]{:S(2)}) async-start(), calls=%async_computation.7 | async-start | bytes 4423680 | tf_op jit(solution)/shard_map/all_gather | solution.py:79
  88.4 0.9 copy-start.1
  107.1 144.8 %reduce-scatter.2.cloned.1.call-start = ((), (), s32[]{:S(2)}) async-start(), calls=%async_computation.6 | async-start | bytes 5898240 | tf_op jit(solution)/shard_map/reduce_scatter | solution.py:92
Sparse Core Ops, SparseCore 0:
  9.1 72.3 all-gather.3
  107.2 45.5 all-gather.5
  188.0 63.8 reduce-scatter.1
